TPU v7x, 256 devices: a whole 4x4x8 slice. The times are simulated.
256 devices in a mesh: term: 8 (over y, x_hi), sector: 32 (over x_lo, z, core).
Axes of the slice: x: 4 (x_hi: 2, x_lo: 2; x = x_hi * 2 + x_lo), y: 4, z: 8, core: 2. Of those that a mesh axis runs over, the one named last changes fastest.
Arguments:
- psi: float32 [512, 128, 128], P('sector'), may hold values from -6 to 6
- left_env: float32 [32, 512, 128, 128], P('term', 'sector'), may hold values from -0.5 to 0.5
- right_env: float32 [32, 512, 128, 128], P('term', 'sector'), may hold values from -0.09375 to 0.09375
- target: int32 [32, 512], P('term', 'sector'), may hold values from 0 to 511, as said below
Outputs:
- sigma: float32 [512, 128, 128], P('sector', 'term')
Inputs may be any that keep to these rules, and one draw needn't show every extreme that they name: Among the 4 * 16 pairs of terms w in one block of 4 consecutive terms and source blocks s in one block of 16 consecutive blocks, at most 4 have their target in any one block of 16 consecutive target blocks, and exactly 4 do for some such block.
All inputs are finite; a program needn't handle non-finite values.
Results may differ from a plain program's by a relative error of at most 0.0001.
Values sent between devices are 32-bit elements; how exact they have to be, the bound alone decides.
No kernel may reach another device: no remote copies, remote signals or barrier semaphores. Data moves between devices by JAX's collectives and lax.ppermute only.
A program may use at most 128 MiB of HBM per device.

v0:
```python
import functools

import jax
import jax.numpy as jnp
from jax import lax
from jax.experimental import pallas as pl
from jax.experimental.pallas import tpu as pltpu
from jax.sharding import PartitionSpec as P


CAP = 4
GROUP = 8
SENDER_STEPS = 4
SPLIT = 2


def split_dot(a, b):
    rows = a.shape[0]
    a_hi = a.astype(jnp.bfloat16)
    a_lo = (a - a_hi.astype(jnp.float32)).astype(jnp.bfloat16)
    b_hi = b.astype(jnp.bfloat16)
    b_lo = (b - b_hi.astype(jnp.float32)).astype(jnp.bfloat16)
    both = jnp.dot(
        jnp.concatenate([a_hi, a_lo], axis=0), b_hi, preferred_element_type=jnp.float32
    )
    cross = jnp.dot(a_hi, b_lo, preferred_element_type=jnp.float32)
    return both[:rows] + (cross + both[rows:])


def slot_tables(target_part):
    term_count, sector_count = target_part.shape
    item_count = term_count * sector_count
    slot_count = lax.axis_size("sector") * CAP
    flat_target = target_part.reshape(item_count)
    owner_dev = flat_target // sector_count
    local_target = flat_target % sector_count
    item_index = jnp.arange(item_count, dtype=jnp.int32)
    term_index = item_index // sector_count
    earlier = (owner_dev[:, None] == owner_dev[None, :]) & (
        item_index[None, :] < item_index[:, None]
    )
    rank_slot = jnp.sum(earlier.astype(jnp.int32), axis=1)
    slot_index = jnp.minimum(owner_dev * CAP + rank_slot, slot_count - 1).astype(jnp.int32)
    slot_range = jnp.arange(slot_count, dtype=jnp.int32)
    match = slot_index[None, :] == slot_range[:, None]
    occupied = jnp.any(match, axis=1)
    item_of_slot = jnp.sum(jnp.where(match, item_index[None, :], 0), axis=1)
    label_of_item = term_index * sector_count + local_target + 1
    labels = jnp.where(occupied, label_of_item[item_of_slot], 0).astype(jnp.int32)
    return slot_index, compact_order(~occupied), labels


def compact_order(flags):
    count = flags.shape[0]
    first = jnp.cumsum(flags.astype(jnp.int32)) - 1
    rest = jnp.sum(flags.astype(jnp.int32)) + jnp.cumsum((~flags).astype(jnp.int32)) - 1
    position = jnp.where(flags, first, rest)
    spots = jnp.arange(count, dtype=jnp.int32)
    chosen = position[None, :] == spots[:, None]
    return jnp.sum(jnp.where(chosen, spots[None, :], 0), axis=1).astype(jnp.int32)


def sender_kernel(slot_ref, empty_ref, left_ref, psi_ref, out_ref, *, term_count, half):
    terms, sector_count = left_ref.shape[:2]
    width = psi_ref.shape[-1]
    band = width // term_count
    piece = band // SPLIT
    step = pl.program_id(0)
    per_step = sector_count // SENDER_STEPS

    @pl.when(step == 0)
    def _():
        for k in range(out_ref.shape[0] - terms * sector_count):
            out_ref[empty_ref[k]] = jnp.zeros(out_ref.shape[1:], jnp.float32)

    for j in range(per_step):
        source = step * per_step + j
        rows = jnp.concatenate(
            [
                left_ref[w, source, pl.ds(i * band + half * piece, piece), :]
                for w in range(terms)
                for i in range(term_count)
            ],
            axis=0,
        )
        value = split_dot(rows, psi_ref[source])
        for w in range(terms):
            out_ref[slot_ref[w * sector_count + source]] = value[w * piece * term_count:(w + 1) * piece * term_count]


def send_blocks(slot_index, empty_slots, left_env, psi, term_count, half):
    slot_count = empty_slots.shape[0]
    width = psi.shape[-1]
    rows = width // SPLIT
    grid_spec = pltpu.PrefetchScalarGridSpec(
        num_scalar_prefetch=2,
        grid=(SENDER_STEPS,),
        in_specs=[
            pl.BlockSpec(left_env.shape, lambda g, *_: (0, 0, 0, 0)),
            pl.BlockSpec(psi.shape, lambda g, *_: (0, 0, 0)),
        ],
        out_specs=pl.BlockSpec((slot_count, rows, width), lambda g, *_: (0, 0, 0)),
    )
    return pl.pallas_call(
        functools.partial(sender_kernel, term_count=term_count, half=half),
        grid_spec=grid_spec,
        out_shape=jax.ShapeDtypeStruct((slot_count, rows, width), jnp.float32),
        compiler_params=pltpu.CompilerParams(vmem_limit_bytes=48 * 1024 * 1024),
    )(slot_index, empty_slots, left_env, psi)


def receiver_kernel(order_ref, count_ref, label_ref, incoming_ref, right_ref, out_ref):
    sector_count = out_ref.shape[0]
    out_ref[...] = jnp.zeros(out_ref.shape, jnp.float32)

    def body(g, carry):
        targets = []
        values = []
        for j in range(GROUP):
            slot = order_ref[g * GROUP + j]
            pair = jnp.maximum(label_ref[slot] - 1, 0)
            term = pair // sector_count
            tgt = pair % sector_count
            targets.append(tgt)
            values.append(split_dot(incoming_ref[slot], right_ref[term, tgt]))
        for tgt, value in zip(targets, values):
            out_ref[tgt] += value
        return carry

    lax.fori_loop(0, (count_ref[0] + GROUP - 1) // GROUP, body, 0)


def receive_blocks(labels, incoming, right_env):
    sector_count = right_env.shape[1]
    _, rows, width = incoming.shape
    occupied = labels > 0
    order = compact_order(occupied)
    count = jnp.sum(occupied.astype(jnp.int32)).reshape(1)
    grid_spec = pltpu.PrefetchScalarGridSpec(
        num_scalar_prefetch=3,
        grid=(1,),
        in_specs=[
            pl.BlockSpec(incoming.shape, lambda g, *_: (0, 0, 0)),
            pl.BlockSpec(right_env.shape, lambda g, *_: (0, 0, 0, 0)),
        ],
        out_specs=pl.BlockSpec((sector_count, rows, width), lambda g, *_: (0, 0, 0)),
    )
    return pl.pallas_call(
        receiver_kernel,
        grid_spec=grid_spec,
        out_shape=jax.ShapeDtypeStruct((sector_count, rows, width), jnp.float32),
        compiler_params=pltpu.CompilerParams(vmem_limit_bytes=48 * 1024 * 1024),
    )(order, count, labels, incoming, right_env)


def term_exchange(partial_value, term_count):
    sector_count, rows, width = partial_value.shape
    pairs_count = term_count // 2
    pieces = partial_value.reshape(sector_count, pairs_count, 2, rows // term_count, width)
    mine = lax.axis_index("term")
    ring = mine // 2
    side = mine % 2
    keep = lax.dynamic_index_in_dim(pieces, side, axis=2, keepdims=False)
    away = lax.dynamic_index_in_dim(pieces, 1 - side, axis=2, keepdims=False)
    partner = [(dev, dev ^ 1) for dev in range(term_count)]
    merged = keep + lax.ppermute(away, "term", partner)
    total = lax.dynamic_index_in_dim(merged, ring, axis=1, keepdims=False)
    for shift in range(1, pairs_count):
        sent = lax.dynamic_index_in_dim(merged, (ring + shift) % pairs_count, axis=1, keepdims=False)
        pairs = [
            (dev, 2 * ((dev // 2 + shift) % pairs_count) + dev % 2) for dev in range(term_count)
        ]
        total = total + lax.ppermute(sent, "term", pairs)
    return total


def on_device_body(psi, left_env, right_env, target):
    term_count = lax.axis_size("term")
    slot_index, empty_slots, labels = slot_tables(target)
    labels_in = lax.all_to_all(labels, "sector", split_axis=0, concat_axis=0, tiled=True)
    results = []
    for half in range(SPLIT):
        piece_out = send_blocks(slot_index, empty_slots, left_env, psi, term_count, half)
        incoming = lax.all_to_all(piece_out, "sector", split_axis=0, concat_axis=0, tiled=True)
        partial_value = receive_blocks(labels_in, incoming, right_env)
        results.append(term_exchange(partial_value, term_count))
    return jnp.concatenate(results, axis=1)


def solution(mesh):
    in_specs = (
        P("sector", None, None),
        P("term", "sector", None, None),
        P("term", "sector", None, None),
        P("term", "sector"),
    )
    out_specs = P("sector", "term", None)
    return jax.shard_map(
        on_device_body, mesh=mesh, in_specs=in_specs, out_specs=out_specs, check_vma=False
    )
```

profile of v0, /device:TPU:96, one launch (start us, length us, event | category | flops | bytes accessed | tf_op | source)
XLA Modules:
  0.0 254.4 jit_solution(3817863460766146157)
XLA Ops:
  0.0 0.8 reshape.276
  0.8 0.2 convert_reduce_fusion
  1.0 0.1 fusion.4
  1.1 0.1 select_reduce_fusion.2
  1.2 0.6 fusion.14
  1.8 0.1 copy.30
  1.9 0.1 copy.29
  2.0 0.2 reduce-window.35
  2.2 0.2 reduce-window.34
  2.4 1.2 gather_fusion
  3.6 0.8 add_reduce_fusion
  4.4 0.7 select_n.141
  5.1 8.7 %all-to-all-start = ((s32[32,4,1]{1,2,0:T(1,128)}), s32[32,4,1]{1,2,0:T(1,128)S(1)}, u32[]{:S(2)}, u32[]{:S(2)}) async-start(s32[32,4,1]{1,2,0:T(1,128)} %bitcast.2), calls=%async_computation | async-start | bytes 32768 | tf_op jit(solution)/shard_map/all_to_all | solution.py:180
  13.9 0.1 select_reduce_fusion.empty_ref
  14.0 0.0 copy-start.2
  14.0 1.2 copy-done.2
  15.2 4.4 %shard_map.48 = f32[128,64,128]{2,1,0:T(8,128)S(1)} custom-call(s32[64]{0:T(128)S(1)} %add_minimum_fusion.slot_ref, s32[128]{0:T(128)S(1)} %select_reduce_fusion.empty_ref, f32[4,16,128,128]{3,2,1,0:T(8,128)} %left_ref.3, f32[16,128,128]{2,1,0:T(8,128)S(1)} %copy-done.2), custom_call_target="tpu_custom_call" | custom-call | tf_op jit(solution)/shard_map/pallas_call | solution.py:104
  19.6 0.0 copy-start.1
  19.6 2.0 copy-done.1
  21.6 0.0 copy-start.3
  21.6 0.0 all-to-all-done
  21.6 8.5 %all-to-all-start.2 = ((f32[128,64,128]{2,1,0:T(8,128)}), f32[128,64,128]{2,1,0:T(8,128)}, u32[]{:S(2)}, u32[]{:S(2)}) async-start(f32[128,64,128]{2,1,0:T(8,128)} %copy-done.1), calls=%async_computation.2 | async-start | bytes 8388608 | tf_op jit(solution)/shard_map/all_to_all | solution.py:184
  30.1 0.0 copy-done.3
  30.1 4.4 %shard_map.46 = f32[128,64,128]{2,1,0:T(8,128)S(1)} custom-call(s32[64]{0:T(128)S(1)} %add_minimum_fusion.slot_ref, s32[128]{0:T(128)S(1)} %select_reduce_fusion.empty_ref, f32[4,16,128,128]{3,2,1,0:T(8,128)} %left_ref.3, f32[16,128,128]{2,1,0:T(8,128)S(1)} %copy-done.3), custom_call_target="tpu_custom_call" | custom-call | tf_op jit(solution)/shard_map/pallas_call | solution.py:104
  34.5 0.0 copy-start
  34.5 2.0 copy-done
  36.5 89.6 %all-to-all-done.2.incoming_ref = f32[128,64,128]{2,1,0:T(8,128)} async-done(((f32[128,64,128]{2,1,0:T(8,128)}), f32[128,64,128]{2,1,0:T(8,128)}, u32[]{:S(2)}, u32[]{:S(2)}) %all-to-all-start.2) | async-done | bytes 4194336 | tf_op jit(solution)/shard_map/all_to_all | solution.py:184
  126.0 5.9 %all-to-all-start.1 = ((f32[128,64,128]{2,1,0:T(8,128)}), f32[128,64,128]{2,1,0:T(8,128)}, u32[]{:S(2)}, u32[]{:S(2)}) async-start(f32[128,64,128]{2,1,0:T(8,128)} %copy-done), calls=%async_computation.1 | async-start | bytes 8388608 | tf_op jit(solution)/shard_map/all_to_all | solution.py:184
  131.9 0.5 broadcast.242
  132.4 1.4 fusion.15
  133.8 0.1 all_to_all.12.label_ref
  133.9 0.1 reshape.293
  134.0 0.2 reduce-window.33
  134.2 0.1 reshape.292
  134.2 0.2 reduce-window.32
  134.4 0.1 add_reduce_fusion.3
  134.5 0.8 add_reduce_fusion.2
  135.3 0.1 select_reduce_fusion.1.order_ref
  135.4 7.2 %shard_map.49 = f32[16,64,128]{2,1,0:T(8,128)S(1)} custom-call(s32[128]{0:T(128)S(1)} %select_reduce_fusion.1.order_ref, s32[1]{0:T(128)} %bitcast.3.count_ref, s32[128]{0:T(128)S(1)} %all_to_all.12.label_ref, f32[128,64,128]{2,1,0:T(8,128)} %all-to-all-done.2.incoming_ref, f32[4,16,128,128]{3,2,1,0:T(8,128)} %right_ref.3), custom_call_target="tpu_custom_call" | custom-call | tf_op jit(solution)/shard_map/pallas_call | solution.py:148
  142.6 3.1 %collective-permute-start.4 = (f32[16,4,8,128]{3,2,1,0:T(8,128)S(1)}, f32[16,4,8,128]{3,2,1,0:T(8,128)S(1)}, u32[]{:S(2)}, u32[]{:S(2)}) collective-permute-start(f32[16,4,8,128]{3,2,1,0:T(8,128)S(1)} %dynamic-slice_bitcast_fusion), channel_id=1, source_target_pairs={{0,32},{32,0},{64,96},{96,64},{128,160},{160,128},{192,224},{224,1... | collective-permute-start | bytes 786440 | tf_op jit(solution)/shard_map/ppermute | solution.py:166
  145.7 81.9 %all-to-all-done.1.incoming_ref = f32[128,64,128]{2,1,0:T(8,128)} async-done(((f32[128,64,128]{2,1,0:T(8,128)}), f32[128,64,128]{2,1,0:T(8,128)}, u32[]{:S(2)}, u32[]{:S(2)}) %all-to-all-start.1) | async-done | bytes 4194336 | tf_op jit(solution)/shard_map/all_to_all | solution.py:184
  227.7 7.2 %shard_map.47 = f32[16,64,128]{2,1,0:T(8,128)S(1)} custom-call(s32[128]{0:T(128)S(1)} %select_reduce_fusion.1.order_ref, s32[1]{0:T(128)} %bitcast.3.count_ref, s32[128]{0:T(128)S(1)} %all_to_all.12.label_ref, f32[128,64,128]{2,1,0:T(8,128)} %all-to-all-done.1.incoming_ref, f32[4,16,128,128]{3,2,1,0:T(8,128)} %right_ref.3), custom_call_target="tpu_custom_call" | custom-call | tf_op jit(solution)/shard_map/pallas_call | solution.py:148
  234.9 3.3 %collective-permute-start = (f32[16,4,8,128]{3,2,1,0:T(8,128)S(1)}, f32[16,4,8,128]{3,2,1,0:T(8,128)S(1)}, u32[]{:S(2)}, u32[]{:S(2)}) collective-permute-start(f32[16,4,8,128]{3,2,1,0:T(8,128)S(1)} %dynamic-slice_bitcast_fusion.1), channel_id=1, source_target_pairs={{0,32},{32,0},{64,96},{96,64},{128,160},{160,128},{192,224},{224,1... | collective-permute-start | bytes 786440 | tf_op jit(solution)/shard_map/ppermute | solution.py:166
  238.1 0.0 collective-permute-done.4
  238.2 1.7 collective-permute-start.5
  239.9 1.6 collective-permute-start.7
  241.5 2.0 collective-permute-start.6
  243.5 1.0 collective-permute-done
  244.6 1.7 collective-permute-start.1
  246.3 1.6 collective-permute-start.3
  247.9 0.0 collective-permute-done.5
  247.9 1.7 collective-permute-start.2
  249.6 0.0 collective-permute-done.7
  249.6 0.0 collective-permute-done.6
  249.6 0.5 collective-permute-done.1
  250.1 0.4 collective-permute-done.3
  250.5 3.2 %collective-permute-done.2 = f32[16,8,128]{2,1,0:T(8,128)S(1)} collective-permute-done((f32[16,8,128]{2,1,0:T(8,128)S(1)}, f32[16,8,128]{2,1,0:T(8,128)S(1)}, u32[]{:S(2)}, u32[]{:S(2)}) %collective-permute-start.2) | collective-permute-done | bytes 65568 | tf_op jit(solution)/shard_map/ppermute | solution.py:173
  253.7 0.7 pad_maximum_fusion
  (15 shorter events, 0.3 us)
Async XLA Ops:
  5.1 16.5 %all-to-all-start = ((s32[32,4,1]{1,2,0:T(1,128)}), s32[32,4,1]{1,2,0:T(1,128)S(1)}, u32[]{:S(2)}, u32[]{:S(2)}) async-start(s32[32,4,1]{1,2,0:T(1,128)} %bitcast.2), calls=%async_computation | async-start | bytes 32768 | tf_op jit(solution)/shard_map/all_to_all | solution.py:180
  14.0 1.2 copy-start.2
  19.6 2.0 copy-start.1
  21.6 8.5 %copy-start.3 = (f32[16,128,128]{2,1,0:T(8,128)S(1)}, f32[16,128,128]{2,1,0:T(8,128)}, u32[]{:S(2)}) copy-start(f32[16,128,128]{2,1,0:T(8,128)} %psi_ref.3) | copy-start | bytes 3145732
  21.6 104.5 %all-to-all-start.2 = ((f32[128,64,128]{2,1,0:T(8,128)}), f32[128,64,128]{2,1,0:T(8,128)}, u32[]{:S(2)}, u32[]{:S(2)}) async-start(f32[128,64,128]{2,1,0:T(8,128)} %copy-done.1), calls=%async_computation.2 | async-start | bytes 8388608 | tf_op jit(solution)/shard_map/all_to_all | solution.py:184
  34.5 2.0 copy-start
  126.0 101.6 %all-to-all-start.1 = ((f32[128,64,128]{2,1,0:T(8,128)}), f32[128,64,128]{2,1,0:T(8,128)}, u32[]{:S(2)}, u32[]{:S(2)}) async-start(f32[128,64,128]{2,1,0:T(8,128)} %copy-done), calls=%async_computation.1 | async-start | bytes 8388608 | tf_op jit(solution)/shard_map/all_to_all | solution.py:184
  142.6 95.5 %collective-permute-start.4 = (f32[16,4,8,128]{3,2,1,0:T(8,128)S(1)}, f32[16,4,8,128]{3,2,1,0:T(8,128)S(1)}, u32[]{:S(2)}, u32[]{:S(2)}) collective-permute-start(f32[16,4,8,128]{3,2,1,0:T(8,128)S(1)} %dynamic-slice_bitcast_fusion), channel_id=1, source_target_pairs={{0,32},{32,0},{64,96},{96,64},{128,160},{160,128},{192,224},{224,1... | collective-permute-start | bytes 786440 | tf_op jit(solution)/shard_map/ppermute | solution.py:166
  234.9 9.6 %collective-permute-start = (f32[16,4,8,128]{3,2,1,0:T(8,128)S(1)}, f32[16,4,8,128]{3,2,1,0:T(8,128)S(1)}, u32[]{:S(2)}, u32[]{:S(2)}) collective-permute-start(f32[16,4,8,128]{3,2,1,0:T(8,128)S(1)} %dynamic-slice_bitcast_fusion.1), channel_id=1, source_target_pairs={{0,32},{32,0},{64,96},{96,64},{128,160},{160,128},{192,224},{224,1... | collective-permute-start | bytes 786440 | tf_op jit(solution)/shard_map/ppermute | solution.py:166
  238.2 9.7 %collective-permute-start.5 = (f32[16,8,128]{2,1,0:T(8,128)S(1)}, f32[16,8,128]{2,1,0:T(8,128)S(1)}, u32[]{:S(2)}, u32[]{:S(2)}) collective-permute-start(f32[16,8,128]{2,1,0:T(8,128)S(1)} %get-tuple-element.12), channel_id=1, source_target_pairs={{0,64},{32,96},{64,128},{96,160},{128,192},{160,224},{192,0},{224,... | collective-permute-start | bytes 196616 | tf_op jit(solution)/shard_map/ppermute | solution.py:173
  239.9 9.7 %collective-permute-start.7 = (f32[16,8,128]{2,1,0:T(8,128)S(1)}, f32[16,8,128]{2,1,0:T(8,128)S(1)}, u32[]{:S(2)}, u32[]{:S(2)}) collective-permute-start(f32[16,8,128]{2,1,0:T(8,128)S(1)} %get-tuple-element.13), channel_id=1, source_target_pairs={{0,192},{32,224},{64,0},{96,32},{128,64},{160,96},{192,128},{224,1... | collective-permute-start | bytes 196616 | tf_op jit(solution)/shard_map/ppermute | solution.py:173
  241.5 8.1 %collective-permute-start.6 = (f32[16,8,128]{2,1,0:T(8,128)S(1)}, f32[16,8,128]{2,1,0:T(8,128)S(1)}, u32[]{:S(2)}, u32[]{:S(2)}) collective-permute-start(f32[16,8,128]{2,1,0:T(8,128)S(1)} %get-tuple-element.14), channel_id=1, source_target_pairs={{0,128},{32,160},{64,192},{96,224},{128,0},{160,32},{192,64},{224,... | collective-permute-start | bytes 196616 | tf_op jit(solution)/shard_map/ppermute | solution.py:173
  244.6 5.6 %collective-permute-start.1 = (f32[16,8,128]{2,1,0:T(8,128)S(1)}, f32[16,8,128]{2,1,0:T(8,128)S(1)}, u32[]{:S(2)}, u32[]{:S(2)}) collective-permute-start(f32[16,8,128]{2,1,0:T(8,128)S(1)} %get-tuple-element.9), channel_id=1, source_target_pairs={{0,64},{32,96},{64,128},{96,160},{128,192},{160,224},{192,0},{224,... | collective-permute-start | bytes 196616 | tf_op jit(solution)/shard_map/ppermute | solution.py:173
  246.3 4.3 %collective-permute-start.3 = (f32[16,8,128]{2,1,0:T(8,128)S(1)}, f32[16,8,128]{2,1,0:T(8,128)S(1)}, u32[]{:S(2)}, u32[]{:S(2)}) collective-permute-start(f32[16,8,128]{2,1,0:T(8,128)S(1)} %get-tuple-element.10), channel_id=1, source_target_pairs={{0,192},{32,224},{64,0},{96,32},{128,64},{160,96},{192,128},{224,1... | collective-permute-start | bytes 196616 | tf_op jit(solution)/shard_map/ppermute | solution.py:173
  247.9 5.8 %collective-permute-start.2 = (f32[16,8,128]{2,1,0:T(8,128)S(1)}, f32[16,8,128]{2,1,0:T(8,128)S(1)}, u32[]{:S(2)}, u32[]{:S(2)}) collective-permute-start(f32[16,8,128]{2,1,0:T(8,128)S(1)} %get-tuple-element.11), channel_id=1, source_target_pairs={{0,128},{32,160},{64,192},{96,224},{128,0},{160,32},{192,64},{224,... | collective-permute-start | bytes 196616 | tf_op jit(solution)/shard_map/ppermute | solution.py:173
where the time goes:
time: 255 us; the launch traced here: 254 us
  waiting for transfers between devices  177 us (69%)
  starting transfers between devices  39.8 us (16%)
  Pallas kernels  23.1 us (9%)
  local copies, waits for them, and re-layouts  8.97 us (4%)
  other arithmetic  5.74 us (2%)
    all_to_all x2, waiting for transfers between devices, on_device_body(): lax.all_to_all(piece_out, 'sector', split_axis=0, concat_axis=0, tiled=True)  172 us
    all_to_all x2, starting transfers between devices, on_device_body(): lax.all_to_all(piece_out, 'sector', split_axis=0, concat_axis=0, tiled=True)  14.3 us
    pallas_call x2, Pallas kernels, receive_blocks(): pl.pallas_call(receiver_kernel, grid_spec=grid_spec, out_shape=jax.ShapeD...  14.3 us
    ppermute x6, starting transfers between devices, term_exchange(): total = total + lax.ppermute(sent, 'term', pairs)  10.3 us
    pallas_call x2, Pallas kernels, send_blocks(): pl.pallas_call(functools.partial(sender_kernel, term_count=term_count, ha...  8.78 us
    all_to_all x1, starting transfers between devices, on_device_body(): lax.all_to_all(labels, 'sector', split_axis=0, concat_axis=0, tiled=True)  8.75 us
    ppermute x2, starting transfers between devices, term_exchange(): merged = keep + lax.ppermute(away, 'term', partner)  6.38 us
    unnamed x8, local copies, waits for them, and re-layouts  5.16 us
  transfers between devices with their start and end apart: 11, of which 6 were waited for; matrix products, arithmetic and copies ran while one was open for 1% of the time, Pallas kernels for 9%

commit v1 on v0

--- a/solution.py
+++ b/solution.py
@@ -174,6 +174,14 @@
     return total
 
 
+def term_all_to_all(partial_value, term_count):
+    sector_count, rows, width = partial_value.shape
+    pieces = partial_value.reshape(sector_count, term_count, rows // term_count, width)
+    pieces = pieces.transpose(1, 0, 2, 3)
+    gathered = lax.all_to_all(pieces, "term", split_axis=0, concat_axis=0, tiled=True)
+    return jnp.sum(gathered, axis=0)
+
+
 def on_device_body(psi, left_env, right_env, target):
     term_count = lax.axis_size("term")
     slot_index, empty_slots, labels = slot_tables(target)
@@ -183,7 +191,10 @@
         piece_out = send_blocks(slot_index, empty_slots, left_env, psi, term_count, half)
         incoming = lax.all_to_all(piece_out, "sector", split_axis=0, concat_axis=0, tiled=True)
         partial_value = receive_blocks(labels_in, incoming, right_env)
-        results.append(term_exchange(partial_value, term_count))
+        if half + 1 < SPLIT:
+            results.append(term_exchange(partial_value, term_count))
+        else:
+            results.append(term_all_to_all(partial_value, term_count))
     return jnp.concatenate(results, axis=1)
 
 

time: 255 us -> 257 us (level)
    all_to_all x0 -> x1, starting transfers between devices: none -> 7.1 us  [term_all_to_all(): lax.all_to_all(pieces, 'term', split_axis=0, concat_axis=0, tiled=True)]
    ppermute x6 -> x3, starting transfers between devices: 10.3 us -> 6.23 us  [term_exchange(): total = total + lax.ppermute(sent, 'term', pairs)]
    ppermute x2 -> x1, starting transfers between devices: 6.38 us -> 3.12 us  [term_exchange(): merged = keep + lax.ppermute(away, 'term', partner)]
    ppermute x6 -> x3, waiting for transfers between devices: 4.07 us -> 5.67 us  [term_exchange(): total = total + lax.ppermute(sent, 'term', pairs)]
  transfers between devices with their start and end apart: 11 -> 8, of which waited for: 6 -> 4; matrix products, arithmetic and copies ran while one was open for 1% -> 2% of each run, Pallas kernels for 9% -> 9%
where the time goes in v1:
time: 257 us; the launch traced here: 255 us
  waiting for transfers between devices  177 us (69%)
  starting transfers between devices  39.5 us (15%)
  Pallas kernels  23.1 us (9%)
  local copies, waits for them, and re-layouts  9.74 us (4%)
  other arithmetic  5.7 us (2%)
    all_to_all x2, waiting for transfers between devices, on_device_body(): lax.all_to_all(piece_out, 'sector', split_axis=0, concat_axis=0, tiled=True)  171 us
    all_to_all x2, starting transfers between devices, on_device_body(): lax.all_to_all(piece_out, 'sector', split_axis=0, concat_axis=0, tiled=True)  14.4 us
    pallas_call x2, Pallas kernels, receive_blocks(): pl.pallas_call(receiver_kernel, grid_spec=grid_spec, out_shape=jax.ShapeD...  14.3 us
    pallas_call x2, Pallas kernels, send_blocks(): pl.pallas_call(functools.partial(sender_kernel, term_count=term_count, ha...  8.77 us
    all_to_all x1, starting transfers between devices, on_device_body(): lax.all_to_all(labels, 'sector', split_axis=0, concat_axis=0, tiled=True)  8.75 us
    all_to_all x1, starting transfers between devices, term_all_to_all(): lax.all_to_all(pieces, 'term', split_axis=0, concat_axis=0, tiled=True)  7.1 us
    ppermute x3, starting transfers between devices, term_exchange(): total = total + lax.ppermute(sent, 'term', pairs)  6.23 us
    ppermute x3, waiting for transfers between devices, term_exchange(): total = total + lax.ppermute(sent, 'term', pairs)  5.67 us
  transfers between devices with their start and end apart: 8, of which 4 were waited for; matrix products, arithmetic and copies ran while one was open for 2% of the time, Pallas kernels for 9%

profile of v1, /device:TPU:96, one launch (start us, length us, event | category | flops | bytes accessed | tf_op | source)
XLA Modules:
  0.0 255.5 jit_solution(16465366412100141809)
XLA Ops:
  0.0 0.8 reshape.276
  0.8 0.2 convert_reduce_fusion
  1.0 0.1 fusion.2
  1.1 0.6 fusion.12
  1.7 0.1 select_reduce_fusion.2
  1.8 0.1 copy.26
  1.9 0.1 copy.27
  2.0 0.2 reduce-window.34
  2.2 0.2 reduce-window.35
  2.4 1.2 gather_fusion
  3.6 0.8 add_reduce_fusion
  4.4 0.7 select_n.126
  5.1 8.7 %all-to-all-start = ((s32[32,4,1]{1,2,0:T(1,128)}), s32[32,4,1]{1,2,0:T(1,128)S(1)}, u32[]{:S(2)}, u32[]{:S(2)}) async-start(s32[32,4,1]{1,2,0:T(1,128)} %bitcast.2), calls=%async_computation | async-start | bytes 32768 | tf_op jit(solution)/shard_map/all_to_all | solution.py:188
  13.9 0.1 select_reduce_fusion.empty_ref
  14.0 0.0 copy-start.2
  14.0 1.2 copy-done.2
  15.2 4.4 %shard_map.46 = f32[128,64,128]{2,1,0:T(8,128)S(1)} custom-call(s32[64]{0:T(128)S(1)} %add_minimum_fusion.slot_ref, s32[128]{0:T(128)S(1)} %select_reduce_fusion.empty_ref, f32[4,16,128,128]{3,2,1,0:T(8,128)} %left_ref.3, f32[16,128,128]{2,1,0:T(8,128)S(1)} %copy-done.2), custom_call_target="tpu_custom_call" | custom-call | tf_op jit(solution)/shard_map/pallas_call | solution.py:104
  19.6 0.0 copy-start.1
  19.6 2.0 copy-done.1
  21.6 0.0 copy-start.3
  21.6 0.0 all-to-all-done
  21.6 8.5 %all-to-all-start.1 = ((f32[128,64,128]{2,1,0:T(8,128)}), f32[128,64,128]{2,1,0:T(8,128)}, u32[]{:S(2)}, u32[]{:S(2)}) async-start(f32[128,64,128]{2,1,0:T(8,128)} %copy-done.1), calls=%async_computation.1 | async-start | bytes 8388608 | tf_op jit(solution)/shard_map/all_to_all | solution.py:192
  30.1 0.0 copy-done.3
  30.1 4.4 %shard_map.48 = f32[128,64,128]{2,1,0:T(8,128)S(1)} custom-call(s32[64]{0:T(128)S(1)} %add_minimum_fusion.slot_ref, s32[128]{0:T(128)S(1)} %select_reduce_fusion.empty_ref, f32[4,16,128,128]{3,2,1,0:T(8,128)} %left_ref.3, f32[16,128,128]{2,1,0:T(8,128)S(1)} %copy-done.3), custom_call_target="tpu_custom_call" | custom-call | tf_op jit(solution)/shard_map/pallas_call | solution.py:104
  34.5 0.0 copy-start
  34.5 2.0 copy-done
  36.5 89.6 %all-to-all-done.1.incoming_ref = f32[128,64,128]{2,1,0:T(8,128)} async-done(((f32[128,64,128]{2,1,0:T(8,128)}), f32[128,64,128]{2,1,0:T(8,128)}, u32[]{:S(2)}, u32[]{:S(2)}) %all-to-all-start.1) | async-done | bytes 4194336 | tf_op jit(solution)/shard_map/all_to_all | solution.py:192
  126.0 5.9 %all-to-all-start.2 = ((f32[128,64,128]{2,1,0:T(8,128)}), f32[128,64,128]{2,1,0:T(8,128)}, u32[]{:S(2)}, u32[]{:S(2)}) async-start(f32[128,64,128]{2,1,0:T(8,128)} %copy-done), calls=%async_computation.2 | async-start | bytes 8388608 | tf_op jit(solution)/shard_map/all_to_all | solution.py:192
  131.9 0.5 broadcast.242
  132.4 1.4 fusion.13
  133.8 0.1 reshape.293
  133.9 0.2 reduce-window.33
  134.1 0.1 all_to_all.15.label_ref
  134.2 0.1 reshape.292
  134.2 0.2 reduce-window.32
  134.4 0.1 add_reduce_fusion.3
  134.5 0.8 add_reduce_fusion.2
  135.3 0.1 select_reduce_fusion.1.order_ref
  135.4 7.2 %shard_map.47 = f32[16,64,128]{2,1,0:T(8,128)S(1)} custom-call(s32[128]{0:T(128)S(1)} %select_reduce_fusion.1.order_ref, s32[1]{0:T(128)} %bitcast.3.count_ref, s32[128]{0:T(128)S(1)} %all_to_all.15.label_ref, f32[128,64,128]{2,1,0:T(8,128)} %all-to-all-done.1.incoming_ref, f32[4,16,128,128]{3,2,1,0:T(8,128)} %right_ref.3), custom_call_target="tpu_custom_call" | custom-call | tf_op jit(solution)/shard_map/pallas_call | solution.py:148
  142.6 3.1 %collective-permute-start = (f32[16,4,8,128]{3,2,1,0:T(8,128)S(1)}, f32[16,4,8,128]{3,2,1,0:T(8,128)S(1)}, u32[]{:S(2)}, u32[]{:S(2)}) collective-permute-start(f32[16,4,8,128]{3,2,1,0:T(8,128)S(1)} %dynamic-slice_bitcast_fusion), channel_id=1, source_target_pairs={{0,32},{32,0},{64,96},{96,64},{128,160},{160,128},{192,224},{224,1... | collective-permute-start | bytes 786440 | tf_op jit(solution)/shard_map/ppermute | solution.py:166
  145.8 81.9 %all-to-all-done.2.incoming_ref = f32[128,64,128]{2,1,0:T(8,128)} async-done(((f32[128,64,128]{2,1,0:T(8,128)}), f32[128,64,128]{2,1,0:T(8,128)}, u32[]{:S(2)}, u32[]{:S(2)}) %all-to-all-start.2) | async-done | bytes 4194336 | tf_op jit(solution)/shard_map/all_to_all | solution.py:192
  227.7 7.2 %shard_map.49 = f32[16,64,128]{2,1,0:T(8,128)S(1)} custom-call(s32[128]{0:T(128)S(1)} %select_reduce_fusion.1.order_ref, s32[1]{0:T(128)} %bitcast.3.count_ref, s32[128]{0:T(128)S(1)} %all_to_all.15.label_ref, f32[128,64,128]{2,1,0:T(8,128)} %all-to-all-done.2.incoming_ref, f32[4,16,128,128]{3,2,1,0:T(8,128)} %right_ref.3), custom_call_target="tpu_custom_call" | custom-call | tf_op jit(solution)/shard_map/pallas_call | solution.py:148
  234.8 0.8 copy_bitcast_fusion
  235.7 7.1 %all-to-all-start.3 = ((f32[8,16,8,128]{3,2,1,0:T(8,128)}), f32[8,16,8,128]{3,2,1,0:T(8,128)S(1)}, u32[]{:S(2)}, u32[]{:S(2)}) async-start(f32[8,16,8,128]{3,2,1,0:T(8,128)} %copy_bitcast_fusion), calls=%async_computation.3 | async-start | bytes 1048576 | tf_op jit(solution)/shard_map/all_to_all | solution.py:181
  242.8 0.0 collective-permute-done
  242.8 2.1 collective-permute-start.1
  244.9 2.7 %collective-permute-start.2 = (f32[16,8,128]{2,1,0:T(8,128)S(1)}, f32[16,8,128]{2,1,0:T(8,128)S(1)}, u32[]{:S(2)}, u32[]{:S(2)}) collective-permute-start(f32[16,8,128]{2,1,0:T(8,128)S(1)} %get-tuple-element.11), channel_id=1, source_target_pairs={{0,128},{32,160},{64,192},{96,224},{128,0},{160,32},{192,64},{224,... | collective-permute-start | bytes 196616 | tf_op jit(solution)/shard_map/ppermute | solution.py:173
  247.6 1.5 collective-permute-start.3
  249.1 4.0 %collective-permute-done.1 = f32[16,8,128]{2,1,0:T(8,128)S(1)} collective-permute-done((f32[16,8,128]{2,1,0:T(8,128)S(1)}, f32[16,8,128]{2,1,0:T(8,128)S(1)}, u32[]{:S(2)}, u32[]{:S(2)}) %collective-permute-start.1) | collective-permute-done | bytes 65568 | tf_op jit(solution)/shard_map/ppermute | solution.py:173
  253.0 1.7 collective-permute-done.2
  254.7 0.0 collective-permute-done.3
  254.8 0.0 all-to-all-done.3
  254.8 0.7 pad_maximum_fusion
  (12 shorter events, 0.2 us)
Async XLA Ops:
  5.1 16.5 %all-to-all-start = ((s32[32,4,1]{1,2,0:T(1,128)}), s32[32,4,1]{1,2,0:T(1,128)S(1)}, u32[]{:S(2)}, u32[]{:S(2)}) async-start(s32[32,4,1]{1,2,0:T(1,128)} %bitcast.2), calls=%async_computation | async-start | bytes 32768 | tf_op jit(solution)/shard_map/all_to_all | solution.py:188
  14.0 1.2 copy-start.2
  19.6 2.0 copy-start.1
  21.6 8.5 %copy-start.3 = (f32[16,128,128]{2,1,0:T(8,128)S(1)}, f32[16,128,128]{2,1,0:T(8,128)}, u32[]{:S(2)}) copy-start(f32[16,128,128]{2,1,0:T(8,128)} %psi_ref.3) | copy-start | bytes 3145732
  21.6 104.5 %all-to-all-start.1 = ((f32[128,64,128]{2,1,0:T(8,128)}), f32[128,64,128]{2,1,0:T(8,128)}, u32[]{:S(2)}, u32[]{:S(2)}) async-start(f32[128,64,128]{2,1,0:T(8,128)} %copy-done.1), calls=%async_computation.1 | async-start | bytes 8388608 | tf_op jit(solution)/shard_map/all_to_all | solution.py:192
  34.5 2.0 copy-start
  126.0 101.6 %all-to-all-start.2 = ((f32[128,64,128]{2,1,0:T(8,128)}), f32[128,64,128]{2,1,0:T(8,128)}, u32[]{:S(2)}, u32[]{:S(2)}) async-start(f32[128,64,128]{2,1,0:T(8,128)} %copy-done), calls=%async_computation.2 | async-start | bytes 8388608 | tf_op jit(solution)/shard_map/all_to_all | solution.py:192
  142.6 100.1 %collective-permute-start = (f32[16,4,8,128]{3,2,1,0:T(8,128)S(1)}, f32[16,4,8,128]{3,2,1,0:T(8,128)S(1)}, u32[]{:S(2)}, u32[]{:S(2)}) collective-permute-start(f32[16,4,8,128]{3,2,1,0:T(8,128)S(1)} %dynamic-slice_bitcast_fusion), channel_id=1, source_target_pairs={{0,32},{32,0},{64,96},{96,64},{128,160},{160,128},{192,224},{224,1... | collective-permute-start | bytes 786440 | tf_op jit(solution)/shard_map/ppermute | solution.py:166
  235.7 19.1 %all-to-all-start.3 = ((f32[8,16,8,128]{3,2,1,0:T(8,128)}), f32[8,16,8,128]{3,2,1,0:T(8,128)S(1)}, u32[]{:S(2)}, u32[]{:S(2)}) async-start(f32[8,16,8,128]{3,2,1,0:T(8,128)} %copy_bitcast_fusion), calls=%async_computation.3 | async-start | bytes 1048576 | tf_op jit(solution)/shard_map/all_to_all | solution.py:181
  242.8 10.2 %collective-permute-start.1 = (f32[16,8,128]{2,1,0:T(8,128)S(1)}, f32[16,8,128]{2,1,0:T(8,128)S(1)}, u32[]{:S(2)}, u32[]{:S(2)}) collective-permute-start(f32[16,8,128]{2,1,0:T(8,128)S(1)} %get-tuple-element.9), channel_id=1, source_target_pairs={{0,64},{32,96},{64,128},{96,160},{128,192},{160,224},{192,0},{224,... | collective-permute-start | bytes 196616 | tf_op jit(solution)/shard_map/ppermute | solution.py:173
  244.9 9.8 %collective-permute-start.2 = (f32[16,8,128]{2,1,0:T(8,128)S(1)}, f32[16,8,128]{2,1,0:T(8,128)S(1)}, u32[]{:S(2)}, u32[]{:S(2)}) collective-permute-start(f32[16,8,128]{2,1,0:T(8,128)S(1)} %get-tuple-element.11), channel_id=1, source_target_pairs={{0,128},{32,160},{64,192},{96,224},{128,0},{160,32},{192,64},{224,... | collective-permute-start | bytes 196616 | tf_op jit(solution)/shard_map/ppermute | solution.py:173
  247.6 7.1 %collective-permute-start.3 = (f32[16,8,128]{2,1,0:T(8,128)S(1)}, f32[16,8,128]{2,1,0:T(8,128)S(1)}, u32[]{:S(2)}, u32[]{:S(2)}) collective-permute-start(f32[16,8,128]{2,1,0:T(8,128)S(1)} %get-tuple-element.10), channel_id=1, source_target_pairs={{0,192},{32,224},{64,0},{96,32},{128,64},{160,96},{192,128},{224,1... | collective-permute-start | bytes 196616 | tf_op jit(solution)/shard_map/ppermute | solution.py:173

commit v2 on v1

--- a/solution.py
+++ b/solution.py
@@ -60,7 +60,8 @@
     return jnp.sum(jnp.where(chosen, spots[None, :], 0), axis=1).astype(jnp.int32)
 
 
-def sender_kernel(slot_ref, empty_ref, left_ref, psi_ref, out_ref, *, term_count, half):
+def sender_kernel(slot_ref, empty_ref, left_ref, psi_ref, *refs, term_count, half):
+    out_ref = refs[-1]
     terms, sector_count = left_ref.shape[:2]
     width = psi_ref.shape[-1]
     band = width // term_count
@@ -68,10 +69,16 @@
     step = pl.program_id(0)
     per_step = sector_count // SENDER_STEPS
 
+    def put(slot, value):
+        out_ref[slot // CAP, pl.ds((slot % CAP) * piece * term_count, piece * term_count), :] = value
+
     @pl.when(step == 0)
     def _():
-        for k in range(out_ref.shape[0] - terms * sector_count):
-            out_ref[empty_ref[k]] = jnp.zeros(out_ref.shape[1:], jnp.float32)
+        for k in range(out_ref.shape[0] * CAP - terms * sector_count):
+            put(empty_ref[k], jnp.zeros((piece * term_count, width), jnp.float32))
+        if refs[:-1]:
+            tiles_ref = refs[0]
+            out_ref[:, pl.ds(CAP * piece * term_count, 8), :] = tiles_ref[...]
 
     for j in range(per_step):
         source = step * per_step + j
@@ -85,32 +92,43 @@
         )
         value = split_dot(rows, psi_ref[source])
         for w in range(terms):
-            out_ref[slot_ref[w * sector_count + source]] = value[w * piece * term_count:(w + 1) * piece * term_count]
-
-
-def send_blocks(slot_index, empty_slots, left_env, psi, term_count, half):
+            put(slot_ref[w * sector_count + source], value[w * piece * term_count:(w + 1) * piece * term_count])
+
+
+def send_blocks(slot_index, empty_slots, left_env, psi, term_count, half, tiles):
     slot_count = empty_slots.shape[0]
+    devices = slot_count // CAP
     width = psi.shape[-1]
     rows = width // SPLIT
+    extra = [] if tiles is None else [tiles]
+    height = CAP * rows + (0 if tiles is None else 8)
     grid_spec = pltpu.PrefetchScalarGridSpec(
         num_scalar_prefetch=2,
         grid=(SENDER_STEPS,),
         in_specs=[
             pl.BlockSpec(left_env.shape, lambda g, *_: (0, 0, 0, 0)),
             pl.BlockSpec(psi.shape, lambda g, *_: (0, 0, 0)),
-        ],
-        out_specs=pl.BlockSpec((slot_count, rows, width), lambda g, *_: (0, 0, 0)),
+        ]
+        + [pl.BlockSpec(t.shape, lambda g, *_: (0, 0, 0)) for t in extra],
+        out_specs=pl.BlockSpec((devices, height, width), lambda g, *_: (0, 0, 0)),
     )
     return pl.pallas_call(
         functools.partial(sender_kernel, term_count=term_count, half=half),
         grid_spec=grid_spec,
-        out_shape=jax.ShapeDtypeStruct((slot_count, rows, width), jnp.float32),
+        out_shape=jax.ShapeDtypeStruct((devices, height, width), jnp.float32),
         compiler_params=pltpu.CompilerParams(vmem_limit_bytes=48 * 1024 * 1024),
-    )(slot_index, empty_slots, left_env, psi)
+    )(slot_index, empty_slots, left_env, psi, *extra)
+
+
+def label_tiles(labels, width):
+    devices = labels.shape[0] // CAP
+    values = labels.reshape(devices, CAP).astype(jnp.float32)
+    tiles = jnp.zeros((devices, 8, width), jnp.float32)
+    return tiles.at[:, 0, :CAP].set(values)
 
 
 def receiver_kernel(order_ref, count_ref, label_ref, incoming_ref, right_ref, out_ref):
-    sector_count = out_ref.shape[0]
+    sector_count, rows = out_ref.shape[:2]
     out_ref[...] = jnp.zeros(out_ref.shape, jnp.float32)
 
     def body(g, carry):
@@ -122,7 +140,8 @@
             term = pair // sector_count
             tgt = pair % sector_count
             targets.append(tgt)
-            values.append(split_dot(incoming_ref[slot], right_ref[term, tgt]))
+            block = incoming_ref[slot // CAP, pl.ds((slot % CAP) * rows, rows), :]
+            values.append(split_dot(block, right_ref[term, tgt]))
         for tgt, value in zip(targets, values):
             out_ref[tgt] += value
         return carry
@@ -132,7 +151,8 @@
 
 def receive_blocks(labels, incoming, right_env):
     sector_count = right_env.shape[1]
-    _, rows, width = incoming.shape
+    width = incoming.shape[-1]
+    rows = right_env.shape[-1] // SPLIT
     occupied = labels > 0
     order = compact_order(occupied)
     count = jnp.sum(occupied.astype(jnp.int32)).reshape(1)
@@ -185,11 +205,16 @@
 def on_device_body(psi, left_env, right_env, target):
     term_count = lax.axis_size("term")
     slot_index, empty_slots, labels = slot_tables(target)
-    labels_in = lax.all_to_all(labels, "sector", split_axis=0, concat_axis=0, tiled=True)
+    width = psi.shape[-1]
+    tiles = label_tiles(labels, width)
     results = []
+    labels_in = None
     for half in range(SPLIT):
-        piece_out = send_blocks(slot_index, empty_slots, left_env, psi, term_count, half)
+        piece_out = send_blocks(slot_index, empty_slots, left_env, psi, term_count, half, tiles if half == 0 else None)
         incoming = lax.all_to_all(piece_out, "sector", split_axis=0, concat_axis=0, tiled=True)
+        if labels_in is None:
+            rows = width // SPLIT
+            labels_in = incoming[:, CAP * rows, :CAP].astype(jnp.int32).reshape(-1)
         partial_value = receive_blocks(labels_in, incoming, right_env)
         if half + 1 < SPLIT:
             results.append(term_exchange(partial_value, term_count))
@@ -206,6 +231,4 @@
         P("term", "sector"),
     )
     out_specs = P("sector", "term", None)
-    return jax.shard_map(
-        on_device_body, mesh=mesh, in_specs=in_specs, out_specs=out_specs, check_vma=False
-    )
+    return jax.shard_map(on_device_body, mesh=mesh, in_specs=in_specs, out_specs=out_specs, check_vma=False)

time: 257 us -> 251 us (0.977)
  starting transfers between devices: 39.5 us -> 31.3 us
    all_to_all x1 -> x0, starting transfers between devices: 8.75 us -> none  [on_device_body(): lax.all_to_all(labels, 'sector', split_axis=0, concat_axis=0, tiled=True)]
    unnamed x8 -> x10, local copies, waits for them, and re-layouts: 5.16 us -> 7.55 us
  transfers between devices with their start and end apart: 8 -> 7, of which waited for: 4 -> 4; matrix products, arithmetic and copies ran while one was open for 2% -> 2% of each run, Pallas kernels for 9% -> 7%
where the time goes in v2:
time: 251 us; the launch traced here: 250 us
  waiting for transfers between devices  179 us (71%)
  starting transfers between devices  31.3 us (12%)
  Pallas kernels  22 us (9%)
  local copies, waits for them, and re-layouts  11 us (4%)
  other arithmetic  6.02 us (2%)
    all_to_all x2, waiting for transfers between devices, on_device_body(): lax.all_to_all(piece_out, 'sector', split_axis=0, concat_axis=0, tiled=True)  173 us
    all_to_all x2, starting transfers between devices, on_device_body(): lax.all_to_all(piece_out, 'sector', split_axis=0, concat_axis=0, tiled=True)  14.9 us
    pallas_call x2, Pallas kernels, receive_blocks(): pl.pallas_call(receiver_kernel, grid_spec=grid_spec, out_shape=jax.ShapeD...  12.9 us
    pallas_call x2, Pallas kernels, send_blocks(): pl.pallas_call(functools.partial(sender_kernel, term_count=term_count, ha...  9.13 us
    unnamed x10, local copies, waits for them, and re-layouts  7.55 us
    all_to_all x1, starting transfers between devices, term_all_to_all(): lax.all_to_all(pieces, 'term', split_axis=0, concat_axis=0, tiled=True)  7.06 us
    ppermute x3, starting transfers between devices, term_exchange(): total = total + lax.ppermute(sent, 'term', pairs)  6.23 us
    ppermute x3, waiting for transfers between devices, term_exchange(): total = total + lax.ppermute(sent, 'term', pairs)  5.67 us
  transfers between devices with their start and end apart: 7, of which 4 were waited for; matrix products, arithmetic and copies ran while one was open for 2% of the time, Pallas kernels for 7%

profile of v2, /device:TPU:96, one launch (start us, length us, event | category | flops | bytes accessed | tf_op | source)
XLA Modules:
  0.0 249.6 jit_solution(6494549810969708637)
XLA Ops:
  0.0 0.8 reshape.319
  0.8 0.2 convert_reduce_fusion
  1.0 0.1 fusion.2
  1.1 0.6 fusion.12
  1.7 0.1 select_reduce_fusion.2
  1.8 0.1 copy.25
  1.9 0.1 copy.26
  2.0 0.2 reduce-window.32
  2.2 0.2 reduce-window.33
  2.4 1.2 gather_fusion
  3.6 0.8 add_reduce_fusion.2
  4.4 0.1 select_reduce_fusion.1.empty_ref
  4.5 0.1 convert_element_type.121
  4.6 0.0 copy-start
  4.7 2.2 copy-done
  6.8 0.0 copy-start.3
  6.8 1.2 copy-done.3
  8.1 4.5 %shard_map.46 = f32[32,264,128]{2,1,0:T(8,128)} custom-call(s32[64]{0:T(128)S(1)} %add_minimum_fusion.slot_ref, s32[128]{0:T(128)S(1)} %select_reduce_fusion.1.empty_ref, f32[4,16,128,128]{3,2,1,0:T(8,128)S(1)} %copy-done, f32[16,128,128]{2,1,0:T(8,128)S(1)} %copy-done.3, f32[32,8,128]{2,1,0:T(8,128)S(1)} %scatter.4.refs_0_), custom_call_target="tpu_custom_call" | custom-call | tf_op jit(solution)/shard_map/pallas_call | solution.py:115
  12.5 0.0 copy-start.4
  12.5 8.9 %all-to-all-start = ((f32[32,264,128]{2,1,0:T(8,128)}), f32[32,264,128]{2,1,0:T(8,128)}, u32[]{:S(2)}, u32[]{:S(2)}) async-start(f32[32,264,128]{2,1,0:T(8,128)} %shard_map.46), calls=%async_computation | async-start | bytes 8650752 | tf_op jit(solution)/shard_map/all_to_all | solution.py:214
  21.5 0.0 copy-done.4
  21.5 4.6 %shard_map.48 = f32[32,256,128]{2,1,0:T(8,128)S(1)} custom-call(s32[64]{0:T(128)S(1)} %add_minimum_fusion.slot_ref, s32[128]{0:T(128)S(1)} %select_reduce_fusion.1.empty_ref, f32[4,16,128,128]{3,2,1,0:T(8,128)} %left_ref.3, f32[16,128,128]{2,1,0:T(8,128)S(1)} %copy-done.4), custom_call_target="tpu_custom_call" | custom-call | tf_op jit(solution)/shard_map/pallas_call | solution.py:115
  26.1 0.0 copy-start.2
  26.1 2.0 copy-done.2
  28.1 92.1 %all-to-all-done.incoming_ref = f32[32,264,128]{2,1,0:T(8,128)} async-done(((f32[32,264,128]{2,1,0:T(8,128)}), f32[32,264,128]{2,1,0:T(8,128)}, u32[]{:S(2)}, u32[]{:S(2)}) %all-to-all-start) | async-done | bytes 4325408 | tf_op jit(solution)/shard_map/all_to_all | solution.py:214
  120.2 6.0 %all-to-all-start.1 = ((f32[32,256,128]{2,1,0:T(8,128)}), f32[32,256,128]{2,1,0:T(8,128)}, u32[]{:S(2)}, u32[]{:S(2)}) async-start(f32[32,256,128]{2,1,0:T(8,128)} %copy-done.2), calls=%async_computation.1 | async-start | bytes 8388608 | tf_op jit(solution)/shard_map/all_to_all | solution.py:214
  126.2 1.7 fusion.13
  127.9 0.1 reshape.336
  127.9 0.2 reduce-window.35
  128.1 0.1 reshape.335
  128.2 0.2 reduce-window.34
  128.4 0.1 convert_element_type.123.label_ref
  128.5 0.1 add_reduce_fusion.1
  128.6 0.8 add_reduce_fusion
  129.4 0.1 select_reduce_fusion.order_ref
  129.5 0.0 copy-start.1
  129.5 2.2 copy-done.1
  131.7 5.8 %shard_map.47 = f32[16,64,128]{2,1,0:T(8,128)S(1)} custom-call(s32[128]{0:T(128)S(1)} %select_reduce_fusion.order_ref, s32[1]{0:T(128)} %bitcast.5.count_ref, s32[128]{0:T(128)S(1)} %convert_element_type.123.label_ref, f32[32,264,128]{2,1,0:T(8,128)} %all-to-all-done.incoming_ref, f32[4,16,128,128]{3,2,1,0:T(8,128)S(1)} %copy-done.1), custom_call_target="tpu_custom_call" | custom-call | tf_op jit(solution)/shard_map/pallas_call | solution.py:168
  137.6 3.1 %collective-permute-start = (f32[16,4,8,128]{3,2,1,0:T(8,128)S(1)}, f32[16,4,8,128]{3,2,1,0:T(8,128)S(1)}, u32[]{:S(2)}, u32[]{:S(2)}) collective-permute-start(f32[16,4,8,128]{3,2,1,0:T(8,128)S(1)} %dynamic-slice_bitcast_fusion), channel_id=1, source_target_pairs={{0,32},{32,0},{64,96},{96,64},{128,160},{160,128},{192,224},{224,1... | collective-permute-start | bytes 786440 | tf_op jit(solution)/shard_map/ppermute | solution.py:186
  140.7 81.3 %all-to-all-done.1.incoming_ref = f32[32,256,128]{2,1,0:T(8,128)} async-done(((f32[32,256,128]{2,1,0:T(8,128)}), f32[32,256,128]{2,1,0:T(8,128)}, u32[]{:S(2)}, u32[]{:S(2)}) %all-to-all-start.1) | async-done | bytes 4194336 | tf_op jit(solution)/shard_map/all_to_all | solution.py:214
  221.9 7.1 %shard_map.49 = f32[16,64,128]{2,1,0:T(8,128)S(1)} custom-call(s32[128]{0:T(128)S(1)} %select_reduce_fusion.order_ref, s32[1]{0:T(128)} %bitcast.5.count_ref, s32[128]{0:T(128)S(1)} %convert_element_type.123.label_ref, f32[32,256,128]{2,1,0:T(8,128)} %all-to-all-done.1.incoming_ref, f32[4,16,128,128]{3,2,1,0:T(8,128)} %right_ref.3), custom_call_target="tpu_custom_call" | custom-call | tf_op jit(solution)/shard_map/pallas_call | solution.py:168
  229.0 0.8 copy_bitcast_fusion
  229.8 7.1 %all-to-all-start.2 = ((f32[8,16,8,128]{3,2,1,0:T(8,128)}), f32[8,16,8,128]{3,2,1,0:T(8,128)S(1)}, u32[]{:S(2)}, u32[]{:S(2)}) async-start(f32[8,16,8,128]{3,2,1,0:T(8,128)} %copy_bitcast_fusion), calls=%async_computation.2 | async-start | bytes 1048576 | tf_op jit(solution)/shard_map/all_to_all | solution.py:201
  236.9 0.0 collective-permute-done
  237.0 2.1 collective-permute-start.1
  239.1 2.7 %collective-permute-start.2 = (f32[16,8,128]{2,1,0:T(8,128)S(1)}, f32[16,8,128]{2,1,0:T(8,128)S(1)}, u32[]{:S(2)}, u32[]{:S(2)}) collective-permute-start(f32[16,8,128]{2,1,0:T(8,128)S(1)} %get-tuple-element.23), channel_id=1, source_target_pairs={{0,128},{32,160},{64,192},{96,224},{128,0},{160,32},{192,64},{224,... | collective-permute-start | bytes 196616 | tf_op jit(solution)/shard_map/ppermute | solution.py:193
  241.8 1.5 collective-permute-start.3
  243.2 4.0 %collective-permute-done.1 = f32[16,8,128]{2,1,0:T(8,128)S(1)} collective-permute-done((f32[16,8,128]{2,1,0:T(8,128)S(1)}, f32[16,8,128]{2,1,0:T(8,128)S(1)}, u32[]{:S(2)}, u32[]{:S(2)}) %collective-permute-start.1) | collective-permute-done | bytes 65568 | tf_op jit(solution)/shard_map/ppermute | solution.py:193
  247.2 1.7 collective-permute-done.2
  248.9 0.0 collective-permute-done.3
  248.9 0.0 all-to-all-done.2
  249.0 0.7 pad_maximum_fusion
  (13 shorter events, 0.2 us)
Async XLA Ops:
  4.6 2.2 copy-start
  6.8 1.2 copy-start.3
  12.5 8.9 %copy-start.4 = (f32[16,128,128]{2,1,0:T(8,128)S(1)}, f32[16,128,128]{2,1,0:T(8,128)}, u32[]{:S(2)}) copy-start(f32[16,128,128]{2,1,0:T(8,128)} %psi_ref.3) | copy-start | bytes 3145732
  12.5 107.7 %all-to-all-start = ((f32[32,264,128]{2,1,0:T(8,128)}), f32[32,264,128]{2,1,0:T(8,128)}, u32[]{:S(2)}, u32[]{:S(2)}) async-start(f32[32,264,128]{2,1,0:T(8,128)} %shard_map.46), calls=%async_computation | async-start | bytes 8650752 | tf_op jit(solution)/shard_map/all_to_all | solution.py:214
  26.1 2.0 copy-start.2
  120.2 101.7 %all-to-all-start.1 = ((f32[32,256,128]{2,1,0:T(8,128)}), f32[32,256,128]{2,1,0:T(8,128)}, u32[]{:S(2)}, u32[]{:S(2)}) async-start(f32[32,256,128]{2,1,0:T(8,128)} %copy-done.2), calls=%async_computation.1 | async-start | bytes 8388608 | tf_op jit(solution)/shard_map/all_to_all | solution.py:214
  129.5 2.2 copy-start.1
  137.6 99.3 %collective-permute-start = (f32[16,4,8,128]{3,2,1,0:T(8,128)S(1)}, f32[16,4,8,128]{3,2,1,0:T(8,128)S(1)}, u32[]{:S(2)}, u32[]{:S(2)}) collective-permute-start(f32[16,4,8,128]{3,2,1,0:T(8,128)S(1)} %dynamic-slice_bitcast_fusion), channel_id=1, source_target_pairs={{0,32},{32,0},{64,96},{96,64},{128,160},{160,128},{192,224},{224,1... | collective-permute-start | bytes 786440 | tf_op jit(solution)/shard_map/ppermute | solution.py:186
  229.8 19.1 %all-to-all-start.2 = ((f32[8,16,8,128]{3,2,1,0:T(8,128)}), f32[8,16,8,128]{3,2,1,0:T(8,128)S(1)}, u32[]{:S(2)}, u32[]{:S(2)}) async-start(f32[8,16,8,128]{3,2,1,0:T(8,128)} %copy_bitcast_fusion), calls=%async_computation.2 | async-start | bytes 1048576 | tf_op jit(solution)/shard_map/all_to_all | solution.py:201
  237.0 10.2 %collective-permute-start.1 = (f32[16,8,128]{2,1,0:T(8,128)S(1)}, f32[16,8,128]{2,1,0:T(8,128)S(1)}, u32[]{:S(2)}, u32[]{:S(2)}) collective-permute-start(f32[16,8,128]{2,1,0:T(8,128)S(1)} %get-tuple-element.21), channel_id=1, source_target_pairs={{0,64},{32,96},{64,128},{96,160},{128,192},{160,224},{192,0},{224,... | collective-permute-start | bytes 196616 | tf_op jit(solution)/shard_map/ppermute | solution.py:193
  239.1 9.8 %collective-permute-start.2 = (f32[16,8,128]{2,1,0:T(8,128)S(1)}, f32[16,8,128]{2,1,0:T(8,128)S(1)}, u32[]{:S(2)}, u32[]{:S(2)}) collective-permute-start(f32[16,8,128]{2,1,0:T(8,128)S(1)} %get-tuple-element.23), channel_id=1, source_target_pairs={{0,128},{32,160},{64,192},{96,224},{128,0},{160,32},{192,64},{224,... | collective-permute-start | bytes 196616 | tf_op jit(solution)/shard_map/ppermute | solution.py:193
  241.8 7.1 %collective-permute-start.3 = (f32[16,8,128]{2,1,0:T(8,128)S(1)}, f32[16,8,128]{2,1,0:T(8,128)S(1)}, u32[]{:S(2)}, u32[]{:S(2)}) collective-permute-start(f32[16,8,128]{2,1,0:T(8,128)S(1)} %get-tuple-element.22), channel_id=1, source_target_pairs={{0,192},{32,224},{64,0},{96,32},{128,64},{160,96},{192,128},{224,1... | collective-permute-start | bytes 196616 | tf_op jit(solution)/shard_map/ppermute | solution.py:193

commit v3 on v2

--- a/solution.py
+++ b/solution.py
@@ -9,8 +9,8 @@
 
 
 CAP = 4
-GROUP = 8
-SENDER_STEPS = 4
+GROUP = 16
+SENDER_STEPS = 1
 SPLIT = 2
 
 
@@ -44,9 +44,8 @@
     slot_range = jnp.arange(slot_count, dtype=jnp.int32)
     match = slot_index[None, :] == slot_range[:, None]
     occupied = jnp.any(match, axis=1)
-    item_of_slot = jnp.sum(jnp.where(match, item_index[None, :], 0), axis=1)
     label_of_item = term_index * sector_count + local_target + 1
-    labels = jnp.where(occupied, label_of_item[item_of_slot], 0).astype(jnp.int32)
+    labels = jnp.sum(jnp.where(match, label_of_item[None, :], 0), axis=1).astype(jnp.int32)
     return slot_index, compact_order(~occupied), labels
 
 

time: 251 us -> 248 us (0.988)
  transfers between devices with their start and end apart: 7 -> 7, of which waited for: 4 -> 4; matrix products, arithmetic and copies ran while one was open for 2% -> 2% of each run, Pallas kernels for 7% -> 6%
where the time goes in v3:
time: 248 us; the launch traced here: 247 us
  waiting for transfers between devices  180 us (73%)
  starting transfers between devices  31.6 us (13%)
  Pallas kernels  19.5 us (8%)
  local copies, waits for them, and re-layouts  9.8 us (4%)
  other arithmetic  6.02 us (2%)
    all_to_all x2, waiting for transfers between devices, on_device_body(): lax.all_to_all(piece_out, 'sector', split_axis=0, concat_axis=0, tiled=True)  174 us
    all_to_all x2, starting transfers between devices, on_device_body(): lax.all_to_all(piece_out, 'sector', split_axis=0, concat_axis=0, tiled=True)  14.9 us
    pallas_call x2, Pallas kernels, receive_blocks(): pl.pallas_call(receiver_kernel, grid_spec=grid_spec, out_shape=jax.ShapeD...  11.8 us
    pallas_call x2, Pallas kernels, send_blocks(): pl.pallas_call(functools.partial(sender_kernel, term_count=term_count, ha...  7.72 us
    unnamed x10, local copies, waits for them, and re-layouts  7.55 us
    all_to_all x1, starting transfers between devices, term_all_to_all(): lax.all_to_all(pieces, 'term', split_axis=0, concat_axis=0, tiled=True)  7.25 us
    ppermute x3, starting transfers between devices, term_exchange(): total = total + lax.ppermute(sent, 'term', pairs)  6.23 us
    ppermute x3, waiting for transfers between devices, term_exchange(): total = total + lax.ppermute(sent, 'term', pairs)  5.67 us
  transfers between devices with their start and end apart: 7, of which 4 were waited for; matrix products, arithmetic and copies ran while one was open for 2% of the time, Pallas kernels for 6%

profile of v3, /device:TPU:96, one launch (start us, length us, event | category | flops | bytes accessed | tf_op | source)
XLA Modules:
  0.0 247.3 jit_solution(13773827642250357298)
XLA Ops:
  0.0 0.8 reshape.332
  0.8 0.2 convert_reduce_fusion
  1.0 0.1 fusion.2
  1.1 0.6 fusion.11
  1.7 0.1 copy.25
  1.8 0.1 copy.26
  1.9 0.2 reduce-window.32
  2.1 0.2 reduce-window.33
  2.3 0.8 add_reduce_fusion.2
  3.0 0.1 select_reduce_fusion.1.empty_ref
  3.2 0.1 select_reduce_fusion.2
  3.3 0.1 convert_element_type.121
  3.4 0.0 copy-start
  3.4 2.2 copy-done
  5.6 0.0 copy-start.3
  5.6 1.2 copy-done.3
  6.8 3.8 %shard_map.46 = f32[32,264,128]{2,1,0:T(8,128)} custom-call(s32[64]{0:T(128)S(1)} %add_minimum_fusion.slot_ref, s32[128]{0:T(128)S(1)} %select_reduce_fusion.1.empty_ref, f32[4,16,128,128]{3,2,1,0:T(8,128)S(1)} %copy-done, f32[16,128,128]{2,1,0:T(8,128)S(1)} %copy-done.3, f32[32,8,128]{2,1,0:T(8,128)S(1)} %scatter.4.refs_0_), custom_call_target="tpu_custom_call" | custom-call | tf_op jit(solution)/shard_map/pallas_call | solution.py:114
  10.6 0.0 copy-start.4
  10.6 8.9 %all-to-all-start = ((f32[32,264,128]{2,1,0:T(8,128)}), f32[32,264,128]{2,1,0:T(8,128)}, u32[]{:S(2)}, u32[]{:S(2)}) async-start(f32[32,264,128]{2,1,0:T(8,128)} %shard_map.46), calls=%async_computation | async-start | bytes 8650752 | tf_op jit(solution)/shard_map/all_to_all | solution.py:213
  19.6 0.0 copy-done.4
  19.6 3.9 %shard_map.48 = f32[32,256,128]{2,1,0:T(8,128)S(1)} custom-call(s32[64]{0:T(128)S(1)} %add_minimum_fusion.slot_ref, s32[128]{0:T(128)S(1)} %select_reduce_fusion.1.empty_ref, f32[4,16,128,128]{3,2,1,0:T(8,128)} %left_ref.3, f32[16,128,128]{2,1,0:T(8,128)S(1)} %copy-done.4), custom_call_target="tpu_custom_call" | custom-call | tf_op jit(solution)/shard_map/pallas_call | solution.py:114
  23.5 0.0 copy-start.2
  23.5 2.0 copy-done.2
  25.4 92.8 %all-to-all-done.incoming_ref = f32[32,264,128]{2,1,0:T(8,128)} async-done(((f32[32,264,128]{2,1,0:T(8,128)}), f32[32,264,128]{2,1,0:T(8,128)}, u32[]{:S(2)}, u32[]{:S(2)}) %all-to-all-start) | async-done | bytes 4325408 | tf_op jit(solution)/shard_map/all_to_all | solution.py:213
  118.3 5.9 %all-to-all-start.1 = ((f32[32,256,128]{2,1,0:T(8,128)}), f32[32,256,128]{2,1,0:T(8,128)}, u32[]{:S(2)}, u32[]{:S(2)}) async-start(f32[32,256,128]{2,1,0:T(8,128)} %copy-done.2), calls=%async_computation.1 | async-start | bytes 8388608 | tf_op jit(solution)/shard_map/all_to_all | solution.py:213
  124.3 1.7 fusion.12
  125.9 0.1 reshape.341
  126.0 0.2 reduce-window.35
  126.2 0.1 convert_element_type.123.label_ref
  126.3 0.1 reshape.340
  126.4 0.2 reduce-window.34
  126.6 0.1 add_reduce_fusion.1
  126.7 0.8 add_reduce_fusion
  127.4 0.1 select_reduce_fusion.order_ref
  127.6 0.0 copy-start.1
  127.6 2.2 copy-done.1
  129.8 5.3 %shard_map.47 = f32[16,64,128]{2,1,0:T(8,128)S(1)} custom-call(s32[128]{0:T(128)S(1)} %select_reduce_fusion.order_ref, s32[1]{0:T(128)} %bitcast.3.count_ref, s32[128]{0:T(128)S(1)} %convert_element_type.123.label_ref, f32[32,264,128]{2,1,0:T(8,128)} %all-to-all-done.incoming_ref, f32[4,16,128,128]{3,2,1,0:T(8,128)S(1)} %copy-done.1), custom_call_target="tpu_custom_call" | custom-call | tf_op jit(solution)/shard_map/pallas_call | solution.py:167
  135.1 3.3 %collective-permute-start = (f32[16,4,8,128]{3,2,1,0:T(8,128)S(1)}, f32[16,4,8,128]{3,2,1,0:T(8,128)S(1)}, u32[]{:S(2)}, u32[]{:S(2)}) collective-permute-start(f32[16,4,8,128]{3,2,1,0:T(8,128)S(1)} %dynamic-slice_bitcast_fusion), channel_id=1, source_target_pairs={{0,32},{32,0},{64,96},{96,64},{128,160},{160,128},{192,224},{224,1... | collective-permute-start | bytes 786440 | tf_op jit(solution)/shard_map/ppermute | solution.py:185
  138.4 81.6 %all-to-all-done.1.incoming_ref = f32[32,256,128]{2,1,0:T(8,128)} async-done(((f32[32,256,128]{2,1,0:T(8,128)}), f32[32,256,128]{2,1,0:T(8,128)}, u32[]{:S(2)}, u32[]{:S(2)}) %all-to-all-start.1) | async-done | bytes 4194336 | tf_op jit(solution)/shard_map/all_to_all | solution.py:213
  220.0 6.5 %shard_map.49 = f32[16,64,128]{2,1,0:T(8,128)S(1)} custom-call(s32[128]{0:T(128)S(1)} %select_reduce_fusion.order_ref, s32[1]{0:T(128)} %bitcast.3.count_ref, s32[128]{0:T(128)S(1)} %convert_element_type.123.label_ref, f32[32,256,128]{2,1,0:T(8,128)} %all-to-all-done.1.incoming_ref, f32[4,16,128,128]{3,2,1,0:T(8,128)} %right_ref.3), custom_call_target="tpu_custom_call" | custom-call | tf_op jit(solution)/shard_map/pallas_call | solution.py:167
  226.5 0.8 copy_bitcast_fusion
  227.3 7.2 %all-to-all-start.2 = ((f32[8,16,8,128]{3,2,1,0:T(8,128)}), f32[8,16,8,128]{3,2,1,0:T(8,128)S(1)}, u32[]{:S(2)}, u32[]{:S(2)}) async-start(f32[8,16,8,128]{3,2,1,0:T(8,128)} %copy_bitcast_fusion), calls=%async_computation.2 | async-start | bytes 1048576 | tf_op jit(solution)/shard_map/all_to_all | solution.py:200
  234.6 0.0 collective-permute-done
  234.7 2.1 collective-permute-start.1
  236.8 2.7 %collective-permute-start.2 = (f32[16,8,128]{2,1,0:T(8,128)S(1)}, f32[16,8,128]{2,1,0:T(8,128)S(1)}, u32[]{:S(2)}, u32[]{:S(2)}) collective-permute-start(f32[16,8,128]{2,1,0:T(8,128)S(1)} %get-tuple-element.23), channel_id=1, source_target_pairs={{0,128},{32,160},{64,192},{96,224},{128,0},{160,32},{192,64},{224,... | collective-permute-start | bytes 196616 | tf_op jit(solution)/shard_map/ppermute | solution.py:192
  239.5 1.5 collective-permute-start.3
  240.9 4.0 %collective-permute-done.1 = f32[16,8,128]{2,1,0:T(8,128)S(1)} collective-permute-done((f32[16,8,128]{2,1,0:T(8,128)S(1)}, f32[16,8,128]{2,1,0:T(8,128)S(1)}, u32[]{:S(2)}, u32[]{:S(2)}) %collective-permute-start.1) | collective-permute-done | bytes 65568 | tf_op jit(solution)/shard_map/ppermute | solution.py:192
  244.9 1.7 collective-permute-done.2
  246.6 0.0 collective-permute-done.3
  246.6 0.0 all-to-all-done.2
  246.7 0.7 pad_maximum_fusion
  (12 shorter events, 0.2 us)
Async XLA Ops:
  3.4 2.2 copy-start
  5.6 1.2 copy-start.3
  10.6 8.9 %copy-start.4 = (f32[16,128,128]{2,1,0:T(8,128)S(1)}, f32[16,128,128]{2,1,0:T(8,128)}, u32[]{:S(2)}) copy-start(f32[16,128,128]{2,1,0:T(8,128)} %psi_ref.3) | copy-start | bytes 3145732
  10.6 107.7 %all-to-all-start = ((f32[32,264,128]{2,1,0:T(8,128)}), f32[32,264,128]{2,1,0:T(8,128)}, u32[]{:S(2)}, u32[]{:S(2)}) async-start(f32[32,264,128]{2,1,0:T(8,128)} %shard_map.46), calls=%async_computation | async-start | bytes 8650752 | tf_op jit(solution)/shard_map/all_to_all | solution.py:213
  23.5 2.0 copy-start.2
  118.3 101.7 %all-to-all-start.1 = ((f32[32,256,128]{2,1,0:T(8,128)}), f32[32,256,128]{2,1,0:T(8,128)}, u32[]{:S(2)}, u32[]{:S(2)}) async-start(f32[32,256,128]{2,1,0:T(8,128)} %copy-done.2), calls=%async_computation.1 | async-start | bytes 8388608 | tf_op jit(solution)/shard_map/all_to_all | solution.py:213
  127.6 2.2 copy-start.1
  135.1 99.5 %collective-permute-start = (f32[16,4,8,128]{3,2,1,0:T(8,128)S(1)}, f32[16,4,8,128]{3,2,1,0:T(8,128)S(1)}, u32[]{:S(2)}, u32[]{:S(2)}) collective-permute-start(f32[16,4,8,128]{3,2,1,0:T(8,128)S(1)} %dynamic-slice_bitcast_fusion), channel_id=1, source_target_pairs={{0,32},{32,0},{64,96},{96,64},{128,160},{160,128},{192,224},{224,1... | collective-permute-start | bytes 786440 | tf_op jit(solution)/shard_map/ppermute | solution.py:185
  227.3 19.3 %all-to-all-start.2 = ((f32[8,16,8,128]{3,2,1,0:T(8,128)}), f32[8,16,8,128]{3,2,1,0:T(8,128)S(1)}, u32[]{:S(2)}, u32[]{:S(2)}) async-start(f32[8,16,8,128]{3,2,1,0:T(8,128)} %copy_bitcast_fusion), calls=%async_computation.2 | async-start | bytes 1048576 | tf_op jit(solution)/shard_map/all_to_all | solution.py:200
  234.7 10.2 %collective-permute-start.1 = (f32[16,8,128]{2,1,0:T(8,128)S(1)}, f32[16,8,128]{2,1,0:T(8,128)S(1)}, u32[]{:S(2)}, u32[]{:S(2)}) collective-permute-start(f32[16,8,128]{2,1,0:T(8,128)S(1)} %get-tuple-element.21), channel_id=1, source_target_pairs={{0,64},{32,96},{64,128},{96,160},{128,192},{160,224},{192,0},{224,... | collective-permute-start | bytes 196616 | tf_op jit(solution)/shard_map/ppermute | solution.py:192
  236.8 9.8 %collective-permute-start.2 = (f32[16,8,128]{2,1,0:T(8,128)S(1)}, f32[16,8,128]{2,1,0:T(8,128)S(1)}, u32[]{:S(2)}, u32[]{:S(2)}) collective-permute-start(f32[16,8,128]{2,1,0:T(8,128)S(1)} %get-tuple-element.23), channel_id=1, source_target_pairs={{0,128},{32,160},{64,192},{96,224},{128,0},{160,32},{192,64},{224,... | collective-permute-start | bytes 196616 | tf_op jit(solution)/shard_map/ppermute | solution.py:192
  239.5 7.1 %collective-permute-start.3 = (f32[16,8,128]{2,1,0:T(8,128)S(1)}, f32[16,8,128]{2,1,0:T(8,128)S(1)}, u32[]{:S(2)}, u32[]{:S(2)}) collective-permute-start(f32[16,8,128]{2,1,0:T(8,128)S(1)} %get-tuple-element.22), channel_id=1, source_target_pairs={{0,192},{32,224},{64,0},{96,32},{128,64},{160,96},{192,128},{224,1... | collective-permute-start | bytes 196616 | tf_op jit(solution)/shard_map/ppermute | solution.py:192

commit v4 on v3

--- a/solution.py
+++ b/solution.py
@@ -172,33 +172,24 @@
     )(order, count, labels, incoming, right_env)
 
 
-def term_exchange(partial_value, term_count):
+def term_exchange_ring_first(partial_value, term_count):
     sector_count, rows, width = partial_value.shape
     pairs_count = term_count // 2
     pieces = partial_value.reshape(sector_count, pairs_count, 2, rows // term_count, width)
     mine = lax.axis_index("term")
     ring = mine // 2
     side = mine % 2
-    keep = lax.dynamic_index_in_dim(pieces, side, axis=2, keepdims=False)
-    away = lax.dynamic_index_in_dim(pieces, 1 - side, axis=2, keepdims=False)
-    partner = [(dev, dev ^ 1) for dev in range(term_count)]
-    merged = keep + lax.ppermute(away, "term", partner)
-    total = lax.dynamic_index_in_dim(merged, ring, axis=1, keepdims=False)
+    merged = lax.dynamic_index_in_dim(pieces, ring, axis=1, keepdims=False)
     for shift in range(1, pairs_count):
-        sent = lax.dynamic_index_in_dim(merged, (ring + shift) % pairs_count, axis=1, keepdims=False)
+        sent = lax.dynamic_index_in_dim(pieces, (ring + shift) % pairs_count, axis=1, keepdims=False)
         pairs = [
             (dev, 2 * ((dev // 2 + shift) % pairs_count) + dev % 2) for dev in range(term_count)
         ]
-        total = total + lax.ppermute(sent, "term", pairs)
-    return total
-
-
-def term_all_to_all(partial_value, term_count):
-    sector_count, rows, width = partial_value.shape
-    pieces = partial_value.reshape(sector_count, term_count, rows // term_count, width)
-    pieces = pieces.transpose(1, 0, 2, 3)
-    gathered = lax.all_to_all(pieces, "term", split_axis=0, concat_axis=0, tiled=True)
-    return jnp.sum(gathered, axis=0)
+        merged = merged + lax.ppermute(sent, "term", pairs)
+    keep = lax.dynamic_index_in_dim(merged, side, axis=1, keepdims=False)
+    away = lax.dynamic_index_in_dim(merged, 1 - side, axis=1, keepdims=False)
+    partner = [(dev, dev ^ 1) for dev in range(term_count)]
+    return keep + lax.ppermute(away, "term", partner)
 
 
 def on_device_body(psi, left_env, right_env, target):
@@ -215,10 +206,7 @@
             rows = width // SPLIT
             labels_in = incoming[:, CAP * rows, :CAP].astype(jnp.int32).reshape(-1)
         partial_value = receive_blocks(labels_in, incoming, right_env)
-        if half + 1 < SPLIT:
-            results.append(term_exchange(partial_value, term_count))
-        else:
-            results.append(term_all_to_all(partial_value, term_count))
+        results.append(term_exchange_ring_first(partial_value, term_count))
     return jnp.concatenate(results, axis=1)
 
 

time: 248 us -> 245 us (0.988)
  waiting for transfers between devices: 180 us -> 176 us
    ppermute x4 -> x8, starting transfers between devices: 9.5 us -> 17.6 us  [the longest x6 11.8 us: term_exchange_ring_first(): merged = merged + lax.ppermute(sent, 'term', pairs)]
    all_to_all x1 -> x0, starting transfers between devices: 7.25 us -> none  [term_all_to_all(): lax.all_to_all(pieces, 'term', split_axis=0, concat_axis=0, tiled=True)]
    all_to_all x2, waiting for transfers between devices: 174 us -> 172 us  [on_device_body(): lax.all_to_all(piece_out, 'sector', split_axis=0, concat_axis=0, tiled=True)]
    ppermute x4 -> x8, waiting for transfers between devices: 5.67 us -> 4.35 us  [the longest x2 3.33 us: term_exchange_ring_first(): return keep + lax.ppermute(away, 'term', partner)]
  transfers between devices with their start and end apart: 7 -> 10, of which waited for: 4 -> 4; matrix products, arithmetic and copies ran while one was open for 2% -> 1% of each run, Pallas kernels for 6% -> 6%
where the time goes in v4:
time: 245 us; the launch traced here: 244 us
  waiting for transfers between devices  176 us (72%)
  starting transfers between devices  32.5 us (13%)
  Pallas kernels  19.5 us (8%)
  local copies, waits for them, and re-layouts  9.01 us (4%)
  other arithmetic  6.03 us (2%)
    all_to_all x2, waiting for transfers between devices, on_device_body(): lax.all_to_all(piece_out, 'sector', split_axis=0, concat_axis=0, tiled=True)  172 us
    all_to_all x2, starting transfers between devices, on_device_body(): lax.all_to_all(piece_out, 'sector', split_axis=0, concat_axis=0, tiled=True)  14.9 us
    pallas_call x2, Pallas kernels, receive_blocks(): pl.pallas_call(receiver_kernel, grid_spec=grid_spec, out_shape=jax.ShapeD...  11.8 us
    ppermute x6, starting transfers between devices, term_exchange_ring_first(): merged = merged + lax.ppermute(sent, 'term', pairs)  11.8 us
    pallas_call x2, Pallas kernels, send_blocks(): pl.pallas_call(functools.partial(sender_kernel, term_count=term_count, ha...  7.72 us
    unnamed x10, local copies, waits for them, and re-layouts  7.55 us
    ppermute x2, starting transfers between devices, term_exchange_ring_first(): return keep + lax.ppermute(away, 'term', partner)  5.79 us
  transfers between devices with their start and end apart: 10, of which 4 were waited for; matrix products, arithmetic and copies ran while one was open for 1% of the time, Pallas kernels for 6%

profile of v4, /device:TPU:96, one launch (start us, length us, event | category | flops | bytes accessed | tf_op | source)
XLA Modules:
  0.0 243.6 jit_solution(12495047291292421618)
XLA Ops:
  0.0 0.8 reshape.332
  0.8 0.2 convert_reduce_fusion
  1.0 0.1 fusion.4
  1.1 0.6 fusion.13
  1.7 0.1 copy.23
  1.8 0.1 copy.24
  1.9 0.2 reduce-window.32
  2.1 0.2 reduce-window.33
  2.3 0.8 add_reduce_fusion.2
  3.0 0.1 select_reduce_fusion.1.empty_ref
  3.2 0.1 select_reduce_fusion.2
  3.3 0.1 convert_element_type.121
  3.4 0.0 copy-start
  3.4 2.2 copy-done
  5.6 0.0 copy-start.3
  5.6 1.2 copy-done.3
  6.8 3.8 %shard_map.46 = f32[32,264,128]{2,1,0:T(8,128)} custom-call(s32[64]{0:T(128)S(1)} %add_minimum_fusion.slot_ref, s32[128]{0:T(128)S(1)} %select_reduce_fusion.1.empty_ref, f32[4,16,128,128]{3,2,1,0:T(8,128)S(1)} %copy-done, f32[16,128,128]{2,1,0:T(8,128)S(1)} %copy-done.3, f32[32,8,128]{2,1,0:T(8,128)S(1)} %scatter.4.refs_0_), custom_call_target="tpu_custom_call" | custom-call | tf_op jit(solution)/shard_map/pallas_call | solution.py:114
  10.6 0.0 copy-start.4
  10.6 8.9 %all-to-all-start = ((f32[32,264,128]{2,1,0:T(8,128)}), f32[32,264,128]{2,1,0:T(8,128)}, u32[]{:S(2)}, u32[]{:S(2)}) async-start(f32[32,264,128]{2,1,0:T(8,128)} %shard_map.46), calls=%async_computation | async-start | bytes 8650752 | tf_op jit(solution)/shard_map/all_to_all | solution.py:204
  19.6 0.0 copy-done.4
  19.6 3.9 %shard_map.48 = f32[32,256,128]{2,1,0:T(8,128)S(1)} custom-call(s32[64]{0:T(128)S(1)} %add_minimum_fusion.slot_ref, s32[128]{0:T(128)S(1)} %select_reduce_fusion.1.empty_ref, f32[4,16,128,128]{3,2,1,0:T(8,128)} %left_ref.3, f32[16,128,128]{2,1,0:T(8,128)S(1)} %copy-done.4), custom_call_target="tpu_custom_call" | custom-call | tf_op jit(solution)/shard_map/pallas_call | solution.py:114
  23.5 0.0 copy-start.2
  23.5 2.0 copy-done.2
  25.4 92.8 %all-to-all-done.incoming_ref = f32[32,264,128]{2,1,0:T(8,128)} async-done(((f32[32,264,128]{2,1,0:T(8,128)}), f32[32,264,128]{2,1,0:T(8,128)}, u32[]{:S(2)}, u32[]{:S(2)}) %all-to-all-start) | async-done | bytes 4325408 | tf_op jit(solution)/shard_map/all_to_all | solution.py:204
  118.3 5.9 %all-to-all-start.1 = ((f32[32,256,128]{2,1,0:T(8,128)}), f32[32,256,128]{2,1,0:T(8,128)}, u32[]{:S(2)}, u32[]{:S(2)}) async-start(f32[32,256,128]{2,1,0:T(8,128)} %copy-done.2), calls=%async_computation.1 | async-start | bytes 8388608 | tf_op jit(solution)/shard_map/all_to_all | solution.py:204
  124.3 1.7 fusion.14
  126.0 0.1 reshape.341
  126.1 0.2 reduce-window.35
  126.2 0.1 convert_element_type.123.label_ref
  126.4 0.1 reshape.340
  126.4 0.2 reduce-window.34
  126.6 0.1 add_reduce_fusion.1
  126.7 0.8 add_reduce_fusion
  127.5 0.1 select_reduce_fusion.order_ref
  127.6 0.0 copy-start.1
  127.6 2.2 copy-done.1
  129.8 5.3 %shard_map.47 = f32[16,64,128]{2,1,0:T(8,128)S(1)} custom-call(s32[128]{0:T(128)S(1)} %select_reduce_fusion.order_ref, s32[1]{0:T(128)} %bitcast.3.count_ref, s32[128]{0:T(128)S(1)} %convert_element_type.123.label_ref, f32[32,264,128]{2,1,0:T(8,128)} %all-to-all-done.incoming_ref, f32[4,16,128,128]{3,2,1,0:T(8,128)S(1)} %copy-done.1), custom_call_target="tpu_custom_call" | custom-call | tf_op jit(solution)/shard_map/pallas_call | solution.py:167
  135.1 1.7 collective-permute-start
  136.8 3.4 %collective-permute-start.1 = (f32[16,2,8,128]{3,2,1,0:T(8,128)S(1)}, f32[16,2,8,128]{3,2,1,0:T(8,128)S(1)}, u32[]{:S(2)}, u32[]{:S(2)}) collective-permute-start(f32[16,2,8,128]{3,2,1,0:T(8,128)S(1)} %get-tuple-element.22), channel_id=1, source_target_pairs={{0,128},{32,160},{64,192},{96,224},{128,0},{160,32},{192,64},{224,... | collective-permute-start | bytes 393224 | tf_op jit(solution)/shard_map/ppermute | solution.py:188
  140.2 0.9 collective-permute-start.2
  141.0 79.1 %all-to-all-done.1.incoming_ref = f32[32,256,128]{2,1,0:T(8,128)} async-done(((f32[32,256,128]{2,1,0:T(8,128)}), f32[32,256,128]{2,1,0:T(8,128)}, u32[]{:S(2)}, u32[]{:S(2)}) %all-to-all-start.1) | async-done | bytes 4194336 | tf_op jit(solution)/shard_map/all_to_all | solution.py:204
  220.2 6.5 %shard_map.49 = f32[16,64,128]{2,1,0:T(8,128)S(1)} custom-call(s32[128]{0:T(128)S(1)} %select_reduce_fusion.order_ref, s32[1]{0:T(128)} %bitcast.3.count_ref, s32[128]{0:T(128)S(1)} %convert_element_type.123.label_ref, f32[32,256,128]{2,1,0:T(8,128)} %all-to-all-done.1.incoming_ref, f32[4,16,128,128]{3,2,1,0:T(8,128)} %right_ref.3), custom_call_target="tpu_custom_call" | custom-call | tf_op jit(solution)/shard_map/pallas_call | solution.py:167
  226.8 1.7 collective-permute-start.4
  228.4 3.4 %collective-permute-start.5 = (f32[16,2,8,128]{3,2,1,0:T(8,128)S(1)}, f32[16,2,8,128]{3,2,1,0:T(8,128)S(1)}, u32[]{:S(2)}, u32[]{:S(2)}) collective-permute-start(f32[16,2,8,128]{3,2,1,0:T(8,128)S(1)} %get-tuple-element.25), channel_id=1, source_target_pairs={{0,128},{32,160},{64,192},{96,224},{128,0},{160,32},{192,64},{224,... | collective-permute-start | bytes 393224 | tf_op jit(solution)/shard_map/ppermute | solution.py:188
  231.8 0.0 collective-permute-done
  231.8 0.9 collective-permute-start.6
  232.7 0.0 collective-permute-done.1
  232.7 0.0 collective-permute-done.2
  232.7 3.3 %collective-permute-start.3 = (f32[16,8,128]{2,1,0:T(8,128)S(1)}, f32[16,8,128]{2,1,0:T(8,128)S(1)}, u32[]{:S(2)}, u32[]{:S(2)}) collective-permute-start(f32[16,8,128]{2,1,0:T(8,128)S(1)} %dynamic-slice_bitcast_fusion.7), channel_id=1, source_target_pairs={{0,32},{32,0},{64,96},{96,64},{128,160},{160,128},{192,224},{224,1... | collective-permute-start | bytes 196616 | tf_op jit(solution)/shard_map/ppermute | solution.py:192
  236.0 0.0 collective-permute-done.4
  236.0 1.0 collective-permute-done.5
  237.0 0.0 collective-permute-done.6
  237.1 2.5 %collective-permute-start.7 = (f32[16,8,128]{2,1,0:T(8,128)S(1)}, f32[16,8,128]{2,1,0:T(8,128)S(1)}, u32[]{:S(2)}, u32[]{:S(2)}) collective-permute-start(f32[16,8,128]{2,1,0:T(8,128)S(1)} %dynamic-slice_bitcast_fusion.6), channel_id=1, source_target_pairs={{0,32},{32,0},{64,96},{96,64},{128,160},{160,128},{192,224},{224,1... | collective-permute-start | bytes 196616 | tf_op jit(solution)/shard_map/ppermute | solution.py:192
  239.6 0.0 collective-permute-done.3
  239.6 3.3 %collective-permute-done.7 = f32[16,8,128]{2,1,0:T(8,128)S(1)} collective-permute-done((f32[16,8,128]{2,1,0:T(8,128)S(1)}, f32[16,8,128]{2,1,0:T(8,128)S(1)}, u32[]{:S(2)}, u32[]{:S(2)}) %collective-permute-start.7) | collective-permute-done | bytes 65568 | tf_op jit(solution)/shard_map/ppermute | solution.py:192
  243.0 0.7 pad_maximum_fusion
  (15 shorter events, 0.3 us)
Async XLA Ops:
  3.4 2.2 copy-start
  5.6 1.2 copy-start.3
  10.6 8.9 %copy-start.4 = (f32[16,128,128]{2,1,0:T(8,128)S(1)}, f32[16,128,128]{2,1,0:T(8,128)}, u32[]{:S(2)}) copy-start(f32[16,128,128]{2,1,0:T(8,128)} %psi_ref.3) | copy-start | bytes 3145732
  10.6 107.7 %all-to-all-start = ((f32[32,264,128]{2,1,0:T(8,128)}), f32[32,264,128]{2,1,0:T(8,128)}, u32[]{:S(2)}, u32[]{:S(2)}) async-start(f32[32,264,128]{2,1,0:T(8,128)} %shard_map.46), calls=%async_computation | async-start | bytes 8650752 | tf_op jit(solution)/shard_map/all_to_all | solution.py:204
  23.5 2.0 copy-start.2
  118.3 101.9 %all-to-all-start.1 = ((f32[32,256,128]{2,1,0:T(8,128)}), f32[32,256,128]{2,1,0:T(8,128)}, u32[]{:S(2)}, u32[]{:S(2)}) async-start(f32[32,256,128]{2,1,0:T(8,128)} %copy-done.2), calls=%async_computation.1 | async-start | bytes 8388608 | tf_op jit(solution)/shard_map/all_to_all | solution.py:204
  127.6 2.2 copy-start.1
  135.1 96.6 %collective-permute-start = (f32[16,2,8,128]{3,2,1,0:T(8,128)S(1)}, f32[16,2,8,128]{3,2,1,0:T(8,128)S(1)}, u32[]{:S(2)}, u32[]{:S(2)}) collective-permute-start(f32[16,2,8,128]{3,2,1,0:T(8,128)S(1)} %get-tuple-element.21), channel_id=1, source_target_pairs={{0,64},{32,96},{64,128},{96,160},{128,192},{160,224},{192,0},{224,... | collective-permute-start | bytes 393224 | tf_op jit(solution)/shard_map/ppermute | solution.py:188
  136.8 95.9 %collective-permute-start.1 = (f32[16,2,8,128]{3,2,1,0:T(8,128)S(1)}, f32[16,2,8,128]{3,2,1,0:T(8,128)S(1)}, u32[]{:S(2)}, u32[]{:S(2)}) collective-permute-start(f32[16,2,8,128]{3,2,1,0:T(8,128)S(1)} %get-tuple-element.22), channel_id=1, source_target_pairs={{0,128},{32,160},{64,192},{96,224},{128,0},{160,32},{192,64},{224,... | collective-permute-start | bytes 393224 | tf_op jit(solution)/shard_map/ppermute | solution.py:188
  140.2 92.5 %collective-permute-start.2 = (f32[16,2,8,128]{3,2,1,0:T(8,128)S(1)}, f32[16,2,8,128]{3,2,1,0:T(8,128)S(1)}, u32[]{:S(2)}, u32[]{:S(2)}) collective-permute-start(f32[16,2,8,128]{3,2,1,0:T(8,128)S(1)} %get-tuple-element.23), channel_id=1, source_target_pairs={{0,192},{32,224},{64,0},{96,32},{128,64},{160,96},{192,128},{224,1... | collective-permute-start | bytes 393224 | tf_op jit(solution)/shard_map/ppermute | solution.py:188
  226.8 9.3 %collective-permute-start.4 = (f32[16,2,8,128]{3,2,1,0:T(8,128)S(1)}, f32[16,2,8,128]{3,2,1,0:T(8,128)S(1)}, u32[]{:S(2)}, u32[]{:S(2)}) collective-permute-start(f32[16,2,8,128]{3,2,1,0:T(8,128)S(1)} %get-tuple-element.24), channel_id=1, source_target_pairs={{0,64},{32,96},{64,128},{96,160},{128,192},{160,224},{192,0},{224,... | collective-permute-start | bytes 393224 | tf_op jit(solution)/shard_map/ppermute | solution.py:188
  228.4 8.6 %collective-permute-start.5 = (f32[16,2,8,128]{3,2,1,0:T(8,128)S(1)}, f32[16,2,8,128]{3,2,1,0:T(8,128)S(1)}, u32[]{:S(2)}, u32[]{:S(2)}) collective-permute-start(f32[16,2,8,128]{3,2,1,0:T(8,128)S(1)} %get-tuple-element.25), channel_id=1, source_target_pairs={{0,128},{32,160},{64,192},{96,224},{128,0},{160,32},{192,64},{224,... | collective-permute-start | bytes 393224 | tf_op jit(solution)/shard_map/ppermute | solution.py:188
  231.8 5.3 %collective-permute-start.6 = (f32[16,2,8,128]{3,2,1,0:T(8,128)S(1)}, f32[16,2,8,128]{3,2,1,0:T(8,128)S(1)}, u32[]{:S(2)}, u32[]{:S(2)}) collective-permute-start(f32[16,2,8,128]{3,2,1,0:T(8,128)S(1)} %get-tuple-element.26), channel_id=1, source_target_pairs={{0,192},{32,224},{64,0},{96,32},{128,64},{160,96},{192,128},{224,1... | collective-permute-start | bytes 393224 | tf_op jit(solution)/shard_map/ppermute | solution.py:188
  232.7 6.9 %collective-permute-start.3 = (f32[16,8,128]{2,1,0:T(8,128)S(1)}, f32[16,8,128]{2,1,0:T(8,128)S(1)}, u32[]{:S(2)}, u32[]{:S(2)}) collective-permute-start(f32[16,8,128]{2,1,0:T(8,128)S(1)} %dynamic-slice_bitcast_fusion.7), channel_id=1, source_target_pairs={{0,32},{32,0},{64,96},{96,64},{128,160},{160,128},{192,224},{224,1... | collective-permute-start | bytes 196616 | tf_op jit(solution)/shard_map/ppermute | solution.py:192
  237.1 5.9 %collective-permute-start.7 = (f32[16,8,128]{2,1,0:T(8,128)S(1)}, f32[16,8,128]{2,1,0:T(8,128)S(1)}, u32[]{:S(2)}, u32[]{:S(2)}) collective-permute-start(f32[16,8,128]{2,1,0:T(8,128)S(1)} %dynamic-slice_bitcast_fusion.6), channel_id=1, source_target_pairs={{0,32},{32,0},{64,96},{96,64},{128,160},{160,128},{192,224},{224,1... | collective-permute-start | bytes 196616 | tf_op jit(solution)/shard_map/ppermute | solution.py:192

commit v5 on v4

--- a/solution.py
+++ b/solution.py
@@ -9,7 +9,7 @@
 
 
 CAP = 4
-GROUP = 16
+GROUP = 8
 SENDER_STEPS = 1
 SPLIT = 2
 
@@ -170,6 +170,27 @@
         out_shape=jax.ShapeDtypeStruct((sector_count, rows, width), jnp.float32),
         compiler_params=pltpu.CompilerParams(vmem_limit_bytes=48 * 1024 * 1024),
     )(order, count, labels, incoming, right_env)
+
+
+def term_exchange(partial_value, term_count):
+    sector_count, rows, width = partial_value.shape
+    pairs_count = term_count // 2
+    pieces = partial_value.reshape(sector_count, pairs_count, 2, rows // term_count, width)
+    mine = lax.axis_index("term")
+    ring = mine // 2
+    side = mine % 2
+    keep = lax.dynamic_index_in_dim(pieces, side, axis=2, keepdims=False)
+    away = lax.dynamic_index_in_dim(pieces, 1 - side, axis=2, keepdims=False)
+    partner = [(dev, dev ^ 1) for dev in range(term_count)]
+    merged = keep + lax.ppermute(away, "term", partner)
+    total = lax.dynamic_index_in_dim(merged, ring, axis=1, keepdims=False)
+    for shift in range(1, pairs_count):
+        sent = lax.dynamic_index_in_dim(merged, (ring + shift) % pairs_count, axis=1, keepdims=False)
+        pairs = [
+            (dev, 2 * ((dev // 2 + shift) % pairs_count) + dev % 2) for dev in range(term_count)
+        ]
+        total = total + lax.ppermute(sent, "term", pairs)
+    return total
 
 
 def term_exchange_ring_first(partial_value, term_count):
@@ -206,7 +227,10 @@
             rows = width // SPLIT
             labels_in = incoming[:, CAP * rows, :CAP].astype(jnp.int32).reshape(-1)
         partial_value = receive_blocks(labels_in, incoming, right_env)
-        results.append(term_exchange_ring_first(partial_value, term_count))
+        if half + 1 < SPLIT:
+            results.append(term_exchange(partial_value, term_count))
+        else:
+            results.append(term_exchange_ring_first(partial_value, term_count))
     return jnp.concatenate(results, axis=1)
 
 

time: 245 us -> 260 us (1.061)
  waiting for transfers between devices: 176 us -> 195 us
  starting transfers between devices: 32.5 us -> 28 us
    all_to_all x2, waiting for transfers between devices: 172 us -> 185 us  [on_device_body(): lax.all_to_all(piece_out, 'sector', split_axis=0, concat_axis=0, tiled=True)]
    ppermute x0 -> x4, waiting for transfers between devices: none -> 9.29 us  [the longest x1 5.72 us: term_exchange(): merged = keep + lax.ppermute(away, 'term', partner)]
    ppermute x0 -> x4, starting transfers between devices: none -> 6.93 us  [the longest x3 3.52 us: term_exchange(): total = total + lax.ppermute(sent, 'term', pairs)]
    ppermute x6 -> x3, starting transfers between devices: 11.8 us -> 5.9 us  [term_exchange_ring_first(): merged = merged + lax.ppermute(sent, 'term', pairs)]
    ppermute x2 -> x1, starting transfers between devices: 5.79 us -> 0.29 us  [term_exchange_ring_first(): return keep + lax.ppermute(away, 'term', partner)]
    ppermute x2 -> x1, waiting for transfers between devices: 3.33 us -> 0.01 us  [term_exchange_ring_first(): return keep + lax.ppermute(away, 'term', partner)]
  transfers between devices with their start and end apart: 10 -> 10, of which waited for: 4 -> 6; matrix products, arithmetic and copies ran while one was open for 1% -> 1% of each run, Pallas kernels for 6% -> 4%
where the time goes in v5:
time: 260 us; the launch traced here: 259 us
  waiting for transfers between devices  195 us (75%)
  starting transfers between devices  28 us (11%)
  Pallas kernels  20.6 us (8%)
  local copies, waits for them, and re-layouts  9.02 us (3%)
  other arithmetic  6.04 us (2%)
    all_to_all x2, waiting for transfers between devices, on_device_body(): lax.all_to_all(piece_out, 'sector', split_axis=0, concat_axis=0, tiled=True)  185 us
    all_to_all x2, starting transfers between devices, on_device_body(): lax.all_to_all(piece_out, 'sector', split_axis=0, concat_axis=0, tiled=True)  14.9 us
    pallas_call x2, Pallas kernels, receive_blocks(): pl.pallas_call(receiver_kernel, grid_spec=grid_spec, out_shape=jax.ShapeD...  12.9 us
    pallas_call x2, Pallas kernels, send_blocks(): pl.pallas_call(functools.partial(sender_kernel, term_count=term_count, ha...  7.72 us
    unnamed x10, local copies, waits for them, and re-layouts  7.55 us
    ppermute x3, starting transfers between devices, term_exchange_ring_first(): merged = merged + lax.ppermute(sent, 'term', pairs)  5.9 us
    ppermute x1, waiting for transfers between devices, term_exchange(): merged = keep + lax.ppermute(away, 'term', partner)  5.72 us
  transfers between devices with their start and end apart: 10, of which 6 were waited for; matrix products, arithmetic and copies ran while one was open for 1% of the time, Pallas kernels for 4%

profile of v5, /device:TPU:96, one launch (start us, length us, event | category | flops | bytes accessed | tf_op | source)
XLA Modules:
  0.0 258.7 jit_solution(5987981205429140809)
XLA Ops:
  0.0 0.8 reshape.332
  0.8 0.2 convert_reduce_fusion
  1.0 0.1 fusion.4
  1.1 0.6 fusion.13
  1.7 0.1 copy.21
  1.8 0.1 copy.22
  1.9 0.2 reduce-window.32
  2.1 0.2 reduce-window.33
  2.3 0.8 add_reduce_fusion.2
  3.0 0.1 select_reduce_fusion.1.empty_ref
  3.2 0.1 select_reduce_fusion.2
  3.3 0.1 convert_element_type.121
  3.4 0.0 copy-start
  3.4 2.2 copy-done
  5.6 0.0 copy-start.3
  5.6 1.2 copy-done.3
  6.8 3.8 %shard_map.46 = f32[32,264,128]{2,1,0:T(8,128)} custom-call(s32[64]{0:T(128)S(1)} %add_minimum_fusion.slot_ref, s32[128]{0:T(128)S(1)} %select_reduce_fusion.1.empty_ref, f32[4,16,128,128]{3,2,1,0:T(8,128)S(1)} %copy-done, f32[16,128,128]{2,1,0:T(8,128)S(1)} %copy-done.3, f32[32,8,128]{2,1,0:T(8,128)S(1)} %scatter.4.refs_0_), custom_call_target="tpu_custom_call" | custom-call | tf_op jit(solution)/shard_map/pallas_call | solution.py:114
  10.6 0.0 copy-start.4
  10.6 8.9 %all-to-all-start = ((f32[32,264,128]{2,1,0:T(8,128)}), f32[32,264,128]{2,1,0:T(8,128)}, u32[]{:S(2)}, u32[]{:S(2)}) async-start(f32[32,264,128]{2,1,0:T(8,128)} %shard_map.46), calls=%async_computation | async-start | bytes 8650752 | tf_op jit(solution)/shard_map/all_to_all | solution.py:225
  19.6 0.0 copy-done.4
  19.6 3.9 %shard_map.48 = f32[32,256,128]{2,1,0:T(8,128)S(1)} custom-call(s32[64]{0:T(128)S(1)} %add_minimum_fusion.slot_ref, s32[128]{0:T(128)S(1)} %select_reduce_fusion.1.empty_ref, f32[4,16,128,128]{3,2,1,0:T(8,128)} %left_ref.3, f32[16,128,128]{2,1,0:T(8,128)S(1)} %copy-done.4), custom_call_target="tpu_custom_call" | custom-call | tf_op jit(solution)/shard_map/pallas_call | solution.py:114
  23.5 0.0 copy-start.2
  23.5 2.0 copy-done.2
  25.4 92.8 %all-to-all-done.incoming_ref = f32[32,264,128]{2,1,0:T(8,128)} async-done(((f32[32,264,128]{2,1,0:T(8,128)}), f32[32,264,128]{2,1,0:T(8,128)}, u32[]{:S(2)}, u32[]{:S(2)}) %all-to-all-start) | async-done | bytes 4325408 | tf_op jit(solution)/shard_map/all_to_all | solution.py:225
  118.3 5.9 %all-to-all-start.1 = ((f32[32,256,128]{2,1,0:T(8,128)}), f32[32,256,128]{2,1,0:T(8,128)}, u32[]{:S(2)}, u32[]{:S(2)}) async-start(f32[32,256,128]{2,1,0:T(8,128)} %copy-done.2), calls=%async_computation.1 | async-start | bytes 8388608 | tf_op jit(solution)/shard_map/all_to_all | solution.py:225
  124.3 1.7 fusion.14
  126.0 0.1 reshape.341
  126.1 0.2 reduce-window.35
  126.2 0.1 convert_element_type.123.label_ref
  126.4 0.1 reshape.340
  126.4 0.2 reduce-window.34
  126.6 0.1 add_reduce_fusion.1
  126.7 0.8 add_reduce_fusion
  127.5 0.1 select_reduce_fusion.order_ref
  127.6 92.6 %all-to-all-done.1.incoming_ref = f32[32,256,128]{2,1,0:T(8,128)} async-done(((f32[32,256,128]{2,1,0:T(8,128)}), f32[32,256,128]{2,1,0:T(8,128)}, u32[]{:S(2)}, u32[]{:S(2)}) %all-to-all-start.1) | async-done | bytes 4194336 | tf_op jit(solution)/shard_map/all_to_all | solution.py:225
  220.2 7.1 %shard_map.49 = f32[16,64,128]{2,1,0:T(8,128)S(1)} custom-call(s32[128]{0:T(128)S(1)} %select_reduce_fusion.order_ref, s32[1]{0:T(128)} %bitcast.3.count_ref, s32[128]{0:T(128)S(1)} %convert_element_type.123.label_ref, f32[32,256,128]{2,1,0:T(8,128)} %all-to-all-done.1.incoming_ref, f32[4,16,128,128]{3,2,1,0:T(8,128)} %right_ref.3), custom_call_target="tpu_custom_call" | custom-call | tf_op jit(solution)/shard_map/pallas_call | solution.py:167
  227.3 1.4 collective-permute-start.4
  228.7 3.5 %collective-permute-start.5 = (f32[16,2,8,128]{3,2,1,0:T(8,128)S(1)}, f32[16,2,8,128]{3,2,1,0:T(8,128)S(1)}, u32[]{:S(2)}, u32[]{:S(2)}) collective-permute-start(f32[16,2,8,128]{3,2,1,0:T(8,128)S(1)} %get-tuple-element.22), channel_id=1, source_target_pairs={{0,128},{32,160},{64,192},{96,224},{128,0},{160,32},{192,64},{224,... | collective-permute-start | bytes 393224 | tf_op jit(solution)/shard_map/ppermute | solution.py:209
  232.2 1.1 collective-permute-start.6
  233.2 0.0 copy-start.1
  233.2 2.2 copy-done.1
  235.4 5.8 %shard_map.47 = f32[16,64,128]{2,1,0:T(8,128)S(1)} custom-call(s32[128]{0:T(128)S(1)} %select_reduce_fusion.order_ref, s32[1]{0:T(128)} %bitcast.3.count_ref, s32[128]{0:T(128)S(1)} %convert_element_type.123.label_ref, f32[32,264,128]{2,1,0:T(8,128)} %all-to-all-done.incoming_ref, f32[4,16,128,128]{3,2,1,0:T(8,128)S(1)} %copy-done.1), custom_call_target="tpu_custom_call" | custom-call | tf_op jit(solution)/shard_map/pallas_call | solution.py:167
  241.3 3.4 %collective-permute-start = (f32[16,4,8,128]{3,2,1,0:T(8,128)S(1)}, f32[16,4,8,128]{3,2,1,0:T(8,128)S(1)}, u32[]{:S(2)}, u32[]{:S(2)}) collective-permute-start(f32[16,4,8,128]{3,2,1,0:T(8,128)S(1)} %dynamic-slice_bitcast_fusion), channel_id=1, source_target_pairs={{0,32},{32,0},{64,96},{96,64},{128,160},{160,128},{192,224},{224,1... | collective-permute-start | bytes 786440 | tf_op jit(solution)/shard_map/ppermute | solution.py:185
  244.7 0.0 collective-permute-done.4
  244.7 0.0 collective-permute-done.5
  244.7 0.0 collective-permute-done.6
  244.8 0.3 collective-permute-start.7
  245.1 5.7 %collective-permute-done = f32[16,4,8,128]{3,2,1,0:T(8,128)S(1)} collective-permute-done((f32[16,4,8,128]{3,2,1,0:T(8,128)S(1)}, f32[16,4,8,128]{3,2,1,0:T(8,128)S(1)}, u32[]{:S(2)}, u32[]{:S(2)}) %collective-permute-start) | collective-permute-done | bytes 262176 | tf_op jit(solution)/shard_map/ppermute | solution.py:185
  250.9 0.7 collective-permute-start.1
  251.6 0.8 collective-permute-start.2
  252.4 2.0 collective-permute-start.3
  254.4 0.0 collective-permute-done.7
  254.4 2.0 collective-permute-done.1
  256.4 1.0 collective-permute-done.2
  257.4 0.6 collective-permute-done.3
  258.0 0.7 pad_maximum_fusion
  (15 shorter events, 0.3 us)
Async XLA Ops:
  3.4 2.2 copy-start
  5.6 1.2 copy-start.3
  10.6 8.9 %copy-start.4 = (f32[16,128,128]{2,1,0:T(8,128)S(1)}, f32[16,128,128]{2,1,0:T(8,128)}, u32[]{:S(2)}) copy-start(f32[16,128,128]{2,1,0:T(8,128)} %psi_ref.3) | copy-start | bytes 3145732
  10.6 107.7 %all-to-all-start = ((f32[32,264,128]{2,1,0:T(8,128)}), f32[32,264,128]{2,1,0:T(8,128)}, u32[]{:S(2)}, u32[]{:S(2)}) async-start(f32[32,264,128]{2,1,0:T(8,128)} %shard_map.46), calls=%async_computation | async-start | bytes 8650752 | tf_op jit(solution)/shard_map/all_to_all | solution.py:225
  23.5 2.0 copy-start.2
  118.3 101.9 %all-to-all-start.1 = ((f32[32,256,128]{2,1,0:T(8,128)}), f32[32,256,128]{2,1,0:T(8,128)}, u32[]{:S(2)}, u32[]{:S(2)}) async-start(f32[32,256,128]{2,1,0:T(8,128)} %copy-done.2), calls=%async_computation.1 | async-start | bytes 8388608 | tf_op jit(solution)/shard_map/all_to_all | solution.py:225
  227.3 17.4 %collective-permute-start.4 = (f32[16,2,8,128]{3,2,1,0:T(8,128)S(1)}, f32[16,2,8,128]{3,2,1,0:T(8,128)S(1)}, u32[]{:S(2)}, u32[]{:S(2)}) collective-permute-start(f32[16,2,8,128]{3,2,1,0:T(8,128)S(1)} %get-tuple-element.21), channel_id=1, source_target_pairs={{0,64},{32,96},{64,128},{96,160},{128,192},{160,224},{192,0},{224,... | collective-permute-start | bytes 393224 | tf_op jit(solution)/shard_map/ppermute | solution.py:209
  228.7 16.0 %collective-permute-start.5 = (f32[16,2,8,128]{3,2,1,0:T(8,128)S(1)}, f32[16,2,8,128]{3,2,1,0:T(8,128)S(1)}, u32[]{:S(2)}, u32[]{:S(2)}) collective-permute-start(f32[16,2,8,128]{3,2,1,0:T(8,128)S(1)} %get-tuple-element.22), channel_id=1, source_target_pairs={{0,128},{32,160},{64,192},{96,224},{128,0},{160,32},{192,64},{224,... | collective-permute-start | bytes 393224 | tf_op jit(solution)/shard_map/ppermute | solution.py:209
  232.2 12.5 %collective-permute-start.6 = (f32[16,2,8,128]{3,2,1,0:T(8,128)S(1)}, f32[16,2,8,128]{3,2,1,0:T(8,128)S(1)}, u32[]{:S(2)}, u32[]{:S(2)}) collective-permute-start(f32[16,2,8,128]{3,2,1,0:T(8,128)S(1)} %get-tuple-element.23), channel_id=1, source_target_pairs={{0,192},{32,224},{64,0},{96,32},{128,64},{160,96},{192,128},{224,1... | collective-permute-start | bytes 393224 | tf_op jit(solution)/shard_map/ppermute | solution.py:209
  233.2 2.2 copy-start.1
  241.3 9.5 %collective-permute-start = (f32[16,4,8,128]{3,2,1,0:T(8,128)S(1)}, f32[16,4,8,128]{3,2,1,0:T(8,128)S(1)}, u32[]{:S(2)}, u32[]{:S(2)}) collective-permute-start(f32[16,4,8,128]{3,2,1,0:T(8,128)S(1)} %dynamic-slice_bitcast_fusion), channel_id=1, source_target_pairs={{0,32},{32,0},{64,96},{96,64},{128,160},{160,128},{192,224},{224,1... | collective-permute-start | bytes 786440 | tf_op jit(solution)/shard_map/ppermute | solution.py:185
  244.8 9.6 %collective-permute-start.7 = (f32[16,8,128]{2,1,0:T(8,128)S(1)}, f32[16,8,128]{2,1,0:T(8,128)S(1)}, u32[]{:S(2)}, u32[]{:S(2)}) collective-permute-start(f32[16,8,128]{2,1,0:T(8,128)S(1)} %dynamic-slice_bitcast_fusion.4), channel_id=1, source_target_pairs={{0,32},{32,0},{64,96},{96,64},{128,160},{160,128},{192,224},{224,1... | collective-permute-start | bytes 196616 | tf_op jit(solution)/shard_map/ppermute | solution.py:213
  250.9 5.6 %collective-permute-start.1 = (f32[16,8,128]{2,1,0:T(8,128)S(1)}, f32[16,8,128]{2,1,0:T(8,128)S(1)}, u32[]{:S(2)}, u32[]{:S(2)}) collective-permute-start(f32[16,8,128]{2,1,0:T(8,128)S(1)} %get-tuple-element.24), channel_id=1, source_target_pairs={{0,64},{32,96},{64,128},{96,160},{128,192},{160,224},{192,0},{224,... | collective-permute-start | bytes 196616 | tf_op jit(solution)/shard_map/ppermute | solution.py:192
  251.6 5.8 %collective-permute-start.2 = (f32[16,8,128]{2,1,0:T(8,128)S(1)}, f32[16,8,128]{2,1,0:T(8,128)S(1)}, u32[]{:S(2)}, u32[]{:S(2)}) collective-permute-start(f32[16,8,128]{2,1,0:T(8,128)S(1)} %get-tuple-element.26), channel_id=1, source_target_pairs={{0,128},{32,160},{64,192},{96,224},{128,0},{160,32},{192,64},{224,... | collective-permute-start | bytes 196616 | tf_op jit(solution)/shard_map/ppermute | solution.py:192
  252.4 5.6 %collective-permute-start.3 = (f32[16,8,128]{2,1,0:T(8,128)S(1)}, f32[16,8,128]{2,1,0:T(8,128)S(1)}, u32[]{:S(2)}, u32[]{:S(2)}) collective-permute-start(f32[16,8,128]{2,1,0:T(8,128)S(1)} %get-tuple-element.25), channel_id=1, source_target_pairs={{0,192},{32,224},{64,0},{96,32},{128,64},{160,96},{192,128},{224,1... | collective-permute-start | bytes 196616 | tf_op jit(solution)/shard_map/ppermute | solution.py:192
